TPU v7x, 512 devices: a whole 4x4x16 slice. The times are simulated.
512 devices in a mesh: var: 16 (over x, z_lo), dp: 32 (over y, z_hi, core).
Axes of the slice: x: 4, y: 4, z: 16 (z_hi: 4, z_lo: 4; z = z_hi * 4 + z_lo), core: 2. Of those that a mesh axis runs over, the one named last changes fastest.
Arguments:
- fields: bfloat16 [32, 64, 32, 128], P('dp', 'var'), may hold values from -6 to 6
- kernels: bfloat16 [64, 16, 512], P('var'), may hold values from -1.5 to 1.5
- level_map: int32 [64], P('var'), may hold values 0 or 1
- norm_gain_vector: float32 [512], replicated, may hold values from 0.1 to 1.9
- w_in: bfloat16 [512, 2048], replicated, may hold values from -0.25 to 0.25
- w_out: bfloat16 [2048, 512], replicated, may hold values from -0.125 to 0.125
- cotangent: bfloat16 [32, 16, 256, 512], P('dp', None, 'var'), may hold values from -6 to 6
Outputs:
- block_out: bfloat16 [32, 16, 256, 512], P('dp', None, 'var')
- kernel_grad: float32 [64, 16, 512], P('var', None, 'dp')
Inputs may be any that keep to these rules, and one draw needn't show every extreme that they name: variable-level v belongs to pressure level v // 4 and enters its aggregate where level_map[v] is 1.
All inputs are finite; a program needn't handle non-finite values. No bound on the sum of `level_map` on one device may be relied on, other than what follows from the above.
Results may differ from a plain program's by a relative error of at most 0.013.
Values may be sent and summed in bfloat16 or wider, within the bound.
No kernel may reach another device: no remote copies, remote signals or barrier semaphores. Data moves between devices by JAX's collectives and lax.ppermute only.
A program may use at most 64 MiB of HBM per device.

v0:
```python
import jax
import jax.numpy as jnp
from jax import lax
from jax.sharding import PartitionSpec as P

PATCH = 4


def patches_of(images):
    batch, count_v, height, width = images.shape
    shaped = images.reshape(batch, count_v, height // PATCH, PATCH, width // PATCH, PATCH)
    return shaped.transpose(0, 1, 2, 4, 3, 5).reshape(
        batch, count_v, height // PATCH * (width // PATCH), PATCH * PATCH
    )


def block_pass(token_rows, grads, norm_gain_vector, w_in, w_out):
    width = token_rows.shape[-1]
    rows = token_rows.reshape(-1, width).astype(jnp.float32)
    mean_row = jnp.mean(rows, axis=1, keepdims=True)
    centered_rows = rows - mean_row
    reciprocal_std = lax.rsqrt(
        jnp.mean(centered_rows * centered_rows, axis=1, keepdims=True) + 1e-05
    )
    normalized_input = centered_rows * reciprocal_std
    normalized_rows = (normalized_input * norm_gain_vector).astype(jnp.bfloat16)
    pre = jnp.dot(normalized_rows, w_in, preferred_element_type=jnp.float32)
    hidden = jax.nn.gelu(pre, approximate=True).astype(jnp.bfloat16)
    output = (rows + jnp.dot(hidden, w_out, preferred_element_type=jnp.float32)).astype(
        jnp.bfloat16
    )
    gradient_rows = grads.reshape(-1, width)
    dhid = jnp.dot(gradient_rows, w_out.T, preferred_element_type=jnp.float32)
    gelu_back = jax.vjp(lambda value: jax.nn.gelu(value, approximate=True), pre)[1]
    dpre = gelu_back(dhid)[0].astype(jnp.bfloat16)
    dnorm = jnp.dot(dpre, w_in.T, preferred_element_type=jnp.float32)
    normalized_gradient = dnorm * norm_gain_vector
    token_gradient = gradient_rows.astype(jnp.float32) + reciprocal_std * (
        normalized_gradient
        - jnp.mean(normalized_gradient, axis=1, keepdims=True)
        - normalized_input * jnp.mean(normalized_gradient * normalized_input, axis=1, keepdims=True)
    )
    return (
        output.reshape(token_rows.shape),
        token_gradient.astype(jnp.bfloat16).reshape(token_rows.shape),
    )


def level_tables(level, weight, groups):
    onehot = (level[None, :] == jnp.arange(groups, dtype=jnp.int32)[:, None]).astype(
        jnp.float32
    ) * weight[None, :]
    inv = 1.0 / jnp.maximum(jnp.sum(onehot, axis=1), 1.0)
    return (onehot * inv[:, None], inv[level] * weight)


def local(fields, kernels, level_map, norm_gain_vector, w_in, w_out, cotangent):
    batch, var_local = (fields.shape[0], fields.shape[1])
    patch_inputs = patches_of(fields)
    tokens_all = patch_inputs.shape[2]
    scale = float(batch * lax.axis_size("dp") * tokens_all) ** (-0.5)
    own_level = jnp.zeros((var_local,), jnp.int32)
    own_assign, own_member = level_tables(own_level, level_map.astype(jnp.float32), 1)
    patch_embeddings = jnp.einsum(
        "bvnp,vpe->bvne", patch_inputs, kernels, preferred_element_type=jnp.float32
    )
    token_rows = jnp.einsum("lv,bvne->blne", own_assign, patch_embeddings).astype(jnp.bfloat16)
    row_tokens = lax.all_to_all(token_rows, "var", split_axis=2, concat_axis=1, tiled=True)
    block_out, token_gradient = block_pass(row_tokens, cotangent, norm_gain_vector, w_in, w_out)
    dlevel = lax.all_to_all(token_gradient, "var", split_axis=1, concat_axis=2, tiled=True)
    partial_grad = (
        jnp.einsum("bvnp,bne->vpe", patch_inputs, dlevel[:, 0], preferred_element_type=jnp.float32)
        * own_member[:, None, None]
    )
    kernel_grad = lax.psum_scatter(partial_grad, "dp", scatter_dimension=2, tiled=True) * scale
    return (block_out, kernel_grad)


def solution(mesh):
    placed = (
        P("dp", "var", None, None),
        P("var", None, None),
        P("var"),
        P(),
        P(),
        P(),
        P("dp", None, "var", None),
    )
    return jax.shard_map(
        local,
        mesh=mesh,
        in_specs=placed,
        out_specs=(P("dp", None, "var", None), P("var", None, "dp")),
        check_vma=False,
    )
```

profile of v0, /device:TPU:1, one launch (start us, length us, event | category | flops | bytes accessed | tf_op | source)
XLA Modules:
  0.0 182.2 jit_solution(2640362188607401655)
XLA Ops:
  7.2 1.4 convert_reduce_fusion.1
  9.3 3.0 %reshape.106 = bf16[1,4,8,4,32,4]{5,4,3,2,1,0:T(8,128)(2,1)S(1)} reshape(bf16[1,4,32,128]{3,2,1,0:T(8,128)(2,1)} %param.7) | data formatting | bytes 65536 | tf_op jit(solution)/shard_map/reshape | solution.py:11
  12.3 0.9 copy.14
  13.3 0.5 convolution_bitcast_fusion
  13.8 1.8 copy.18
  15.6 1.9 %fusion.47 = bf16[1,256,512]{2,0,1:T(2,128)(2,1)S(1)} fusion(bf16[4,256,512]{2,0,1:T(4,128)(2,1)} %copy.18, f32[]{:T(128)S(6)} %div.16, s32[4]{0:T(128)S(1)} %copy-done.4), kind=kOutput, calls=%fused_computation.62 | convolution fusion | flops 1048584 | bytes 1310740 | tf_op jit(solution)/shard_map/lv,bvne->blne/dot_general | solution.py:67
  17.6 0.4 copy.28
  18.0 0.5 broadcast.100
  18.5 2.3 %reduce.6 = bf16[256,512]{1,0:T(8,128)(2,1)S(1)} reduce(bf16[256,1,1,512]{3,2,1,0:T(2,128)(2,1)S(1)} %bitcast.92, bf16[]{:T(256)} %broadcast.100), dimensions={1,2}, to_apply=%bitcast.88.reduce_sub_computation | reduce | bytes 524290
  20.8 0.2 reshape.120
  21.0 18.7 %all_to_all.8 = bf16[16,2,4096]{2,1,0:T(2,128)(2,1)S(1)} all-to-all(bf16[16,2,4096]{2,1,0:T(2,128)(2,1)S(1)} %reshape.120), channel_id=1, replica_groups=mesh['var'=16,'dp'=32] {'var'}, dimensions={0} | all-to-all | bytes 524288 | tf_op jit(solution)/shard_map/all_to_all | solution.py:68
  39.7 0.3 reshape.121
  40.1 0.2 fusion.24
  40.4 2.2 %fusion.26 = f32[256,2048]{1,0:T(8,128)} fusion(bf16[512,2048]{1,0:T(8,128)(2,1)S(1)} %copy-done, bf16[1,1,256,512]{3,2,1,0:T(8,128)(2,1)S(1)} %get-tuple-element.5, f32[512]{0:T(512)S(1)} %copy-done.3, f32[256]{0:T(256)S(1)} %add_rsqrt_fusion, f32[256]{0:T(256)S(1)} %broadcast_multiply_fusion.3), kind=kOutput, calls=%fused_computation.35 | convolution fusion | flops 537526272 | bytes 4460544 | tf_op jit(solution)/shard_map/dot_general | solution.py:27
  42.5 4.7 %fusion.43 = (f32[256]{0:T(256)S(1)}, f32[256]{0:T(256)S(1)}, f32[256,512]{1,0:T(8,128)S(1)}) fusion(f32[256]{0:T(256)S(1)} %add_rsqrt_fusion, f32[256]{0:T(256)S(1)} %broadcast_multiply_fusion.3, bf16[1,1,256,512]{3,2,1,0:T(8,128)(2,1)S(1)} %get-tuple-element.5, f32[512]{0:T(512)S(1)} %copy-done.3, bf16[512,2048]{1,0:T(8,128)(2,1)S(1)} %copy-done, ...), kind=kOutput, calls=%fused_computation.59 | convolution fusion | flops 1085144576 | bytes 7346176 | tf_op jit(solution)/shard_map/dot_general | solution.py:36
  47.2 1.0 fusion.22
  48.2 3.8 %all-to-all-start.1 = ((bf16[1,16,16,512]{3,2,0,1:T(8,128)(2,1)}), bf16[1,16,16,512]{3,2,0,1:T(8,128)(2,1)S(1)}, u32[]{:S(2)}, u32[]{:S(2)}) async-start(bf16[1,16,16,512]{3,2,0,1:T(8,128)(2,1)} %bitcast.11), calls=%async_computation.1 | async-start | bytes 524288 | tf_op jit(solution)/shard_map/all_to_all | solution.py:70
  52.0 8.6 %all-to-all-done.1 = bf16[1,16,16,512]{3,2,0,1:T(8,128)(2,1)S(1)} async-done(((bf16[1,16,16,512]{3,2,0,1:T(8,128)(2,1)}), bf16[1,16,16,512]{3,2,0,1:T(8,128)(2,1)S(1)}, u32[]{:S(2)}, u32[]{:S(2)}) %all-to-all-start.1) | async-done | bytes 262176 | tf_op jit(solution)/shard_map/all_to_all | solution.py:70
  60.8 0.4 copy.20
  61.2 1.2 reshape.118
  62.4 3.8 %fusion.7 = bf16[256,512]{1,0:T(8,128)(2,1)} fusion(bf16[2048,512]{1,0:T(8,128)(2,1)} %param.12, f32[256,2048]{1,0:T(8,128)} %fusion.26, bf16[1,1,256,512]{3,2,1,0:T(8,128)(2,1)S(1)} %get-tuple-element.5), kind=kOutput, calls=%fused_computation.13 | convolution fusion | flops 541982720 | bytes 4718592 | tf_op jit(solution)/shard_map/dot_general | solution.py:29
  66.2 107.7 %reduce-scatter.4.cloned.1.call-done = f32[16,64]{1,0:T(8,128)} async-done(((f32[512,64]{1,0:T(8,128)}), f32[16,64]{1,0:T(8,128)}) %reduce-scatter.4.cloned.1.call-update) | async-done | bytes 4112
  173.8 0.8 reshape.119
  174.7 0.6 broadcast_multiply_fusion
  (22 shorter events, 0.7 us)
Async XLA Ops:
  7.2 33.2 %copy-start = (bf16[512,2048]{1,0:T(8,128)(2,1)S(1)}, bf16[512,2048]{1,0:T(8,128)(2,1)}, u32[]{:S(2)}) copy-start(bf16[512,2048]{1,0:T(8,128)(2,1)} %param.11) | copy-start | bytes 6291460
  7.2 6.1 %copy-start.2 = (bf16[4,16,512]{2,1,0:T(8,128)(2,1)S(1)}, bf16[4,16,512]{2,1,0:T(8,128)(2,1)}, u32[]{:S(2)}) copy-start(bf16[4,16,512]{2,1,0:T(8,128)(2,1)} %param.8) | copy-start | bytes 196612
  12.3 3.3 %copy-start.4 = (s32[4]{0:T(128)S(1)}, s32[4]{0:T(128)}, u32[]{:S(2)}) copy-start(s32[4]{0:T(128)} %param.9) | copy-start | bytes 52
  17.6 22.8 %copy-start.3 = (f32[512]{0:T(512)S(1)}, f32[512]{0:T(512)}, u32[]{:S(2)}) copy-start(f32[512]{0:T(512)} %param.10) | copy-start | bytes 6148
  40.4 2.2 %copy-start.1 = (bf16[1,16,16,512]{3,2,1,0:T(8,128)(2,1)S(1)}, bf16[1,16,16,512]{3,2,1,0:T(8,128)(2,1)}, u32[]{:S(2)}) copy-start(bf16[1,16,16,512]{3,2,1,0:T(8,128)(2,1)} %param.13) | copy-start | bytes 786436
  48.2 12.4 %all-to-all-start.1 = ((bf16[1,16,16,512]{3,2,0,1:T(8,128)(2,1)}), bf16[1,16,16,512]{3,2,0,1:T(8,128)(2,1)S(1)}, u32[]{:S(2)}, u32[]{:S(2)}) async-start(bf16[1,16,16,512]{3,2,0,1:T(8,128)(2,1)} %bitcast.11), calls=%async_computation.1 | async-start | bytes 524288 | tf_op jit(solution)/shard_map/all_to_all | solution.py:70
  51.9 121.9 %reduce-scatter.4.cloned.1.call-start = ((), (), s32[]{:S(2)}) async-start(), calls=%async_computation.3 | async-start | bytes 270336
Sparse Core Ops, SparseCore 0:
  62.5 111.2 reduce-scatter.3
where the time goes:
time: 184 us; the launch traced here: 182 us
  waiting for transfers between devices  116 us (63%)
  blocking collectives  18.7 us (10%)
  between operations  14.9 us (8%)
  matrix products  13.1 us (7%)
  local copies, waits for them, and re-layouts  9.68 us (5%)
  other arithmetic  5.72 us (3%)
  starting transfers between devices  3.79 us (2%)
    unnamed x2, waiting for transfers between devices  108 us
    all_to_all x1, blocking collectives, local(): lax.all_to_all(token_rows, 'var', split_axis=2, concat_axis=1, tiled=True)  18.7 us
    all_to_all x1, waiting for transfers between devices, local(): lax.all_to_all(token_gradient, 'var', split_axis=1, concat_axis=2, tiled=...  8.55 us
    dot_general x1, matrix products, block_pass(): dnorm = jnp.dot(dpre, w_in.T, preferred_element_type=jnp.float32)  4.66 us
    dot_general x1, matrix products, block_pass(): jnp.dot(hidden, w_out, preferred_element_type=jnp.float32)  3.76 us
    all_to_all x1, starting transfers between devices, local(): lax.all_to_all(token_gradient, 'var', split_axis=1, concat_axis=2, tiled=...  3.75 us
  transfers between devices with their start and end apart: 2, of which 2 were waited for; matrix products, arithmetic and copies ran while one was open for 2% of the time, Pallas kernels for 0%

commit v1 on v0

--- a/solution.py
+++ b/solution.py
@@ -72,7 +72,11 @@
         jnp.einsum("bvnp,bne->vpe", patch_inputs, dlevel[:, 0], preferred_element_type=jnp.float32)
         * own_member[:, None, None]
     )
-    kernel_grad = lax.psum_scatter(partial_grad, "dp", scatter_dimension=2, tiled=True) * scale
+    parts = lax.axis_size("dp")
+    var_n, patch_n, width = partial_grad.shape
+    pieces = partial_grad.reshape(var_n, patch_n, parts, width // parts)
+    gathered = lax.all_to_all(pieces, "dp", split_axis=2, concat_axis=2, tiled=True)
+    kernel_grad = jnp.sum(gathered, axis=2) * scale
     return (block_out, kernel_grad)
 
 

time: 184 us -> 95.4 us (0.52)
  waiting for transfers between devices: 116 us -> 20.5 us
  starting transfers between devices: 3.79 us -> 22.1 us
  between operations: 14.9 us -> 1.53 us
  local copies, waits for them, and re-layouts: 9.68 us -> 12.5 us
    unnamed x2 -> x0, waiting for transfers between devices: 108 us -> none
    all_to_all x0 -> x1, starting transfers between devices: none -> 18.4 us  [local(): lax.all_to_all(pieces, 'dp', split_axis=2, concat_axis=2, tiled=True)]
    all_to_all x0 -> x1, waiting for transfers between devices: none -> 11.9 us  [local(): lax.all_to_all(pieces, 'dp', split_axis=2, concat_axis=2, tiled=True)]
    reshape x1 -> x3, local copies, waits for them, and re-layouts: 0.14 us -> 2.1 us  [the longest x2 1.96 us: local(): pieces = partial_grad.reshape(var_n, patch_n, parts, width // parts)]
  transfers between devices with their start and end apart: 2 -> 2, of which waited for: 2 -> 2; matrix products, arithmetic and copies ran while one was open for 2% -> 4% of each run, Pallas kernels for 0% -> 0%
where the time goes in v1:
time: 95.4 us; the launch traced here: 94.4 us
  starting transfers between devices  22.1 us (23%)
  waiting for transfers between devices  20.5 us (21%)
  blocking collectives  18.7 us (20%)
  matrix products  13.1 us (14%)
  local copies, waits for them, and re-layouts  12.5 us (13%)
  other arithmetic  5.86 us (6%)
  between operations  1.53 us (2%)
    all_to_all x1, blocking collectives, local(): lax.all_to_all(token_rows, 'var', split_axis=2, concat_axis=1, tiled=True)  18.7 us
    all_to_all x1, starting transfers between devices, local(): lax.all_to_all(pieces, 'dp', split_axis=2, concat_axis=2, tiled=True)  18.4 us
    all_to_all x1, waiting for transfers between devices, local(): lax.all_to_all(pieces, 'dp', split_axis=2, concat_axis=2, tiled=True)  11.9 us
    all_to_all x1, waiting for transfers between devices, local(): lax.all_to_all(token_gradient, 'var', split_axis=1, concat_axis=2, tiled=...  8.61 us
    dot_general x1, matrix products, block_pass(): dnorm = jnp.dot(dpre, w_in.T, preferred_element_type=jnp.float32)  4.64 us
    dot_general x1, matrix products, block_pass(): jnp.dot(hidden, w_out, preferred_element_type=jnp.float32)  3.76 us
    all_to_all x1, starting transfers between devices, local(): lax.all_to_all(token_gradient, 'var', split_axis=1, concat_axis=2, tiled=...  3.75 us
    unnamed x15, local copies, waits for them, and re-layouts  3.61 us
  transfers between devices with their start and end apart: 2, of which 2 were waited for; matrix products, arithmetic and copies ran while one was open for 4% of the time, Pallas kernels for 0%

profile of v1, /device:TPU:1, one launch (start us, length us, event | category | flops | bytes accessed | tf_op | source)
XLA Modules:
  0.0 94.4 jit_solution(2193136800449732821)
XLA Ops:
  0.7 3.2 %reshape.109 = bf16[1,4,8,4,32,4]{5,4,3,2,1,0:T(8,128)(2,1)S(1)} reshape(bf16[1,4,32,128]{3,2,1,0:T(8,128)(2,1)} %param.7) | data formatting | bytes 65536 | tf_op jit(solution)/shard_map/reshape | solution.py:11
  3.8 0.9 copy.15
  4.8 0.5 convolution_bitcast_fusion
  5.3 1.8 %copy.20 = bf16[4,256,512]{2,0,1:T(4,128)(2,1)} copy(bf16[4,256,512]{1,2,0:T(8,128)(2,1)S(1)} %convolution_bitcast_fusion) | data formatting | bytes 2097152 | tf_op jit(solution)/shard_map/reshape.3
  7.1 0.6 convert_reduce_fusion.1
  8.4 1.9 %fusion.47 = bf16[1,256,512]{2,0,1:T(2,128)(2,1)S(1)} fusion(bf16[4,256,512]{2,0,1:T(4,128)(2,1)} %copy.20, f32[]{:T(128)S(6)} %div.16, s32[4]{0:T(128)S(1)} %copy-done.4), kind=kOutput, calls=%fused_computation.64 | convolution fusion | flops 1048584 | bytes 1310740 | tf_op jit(solution)/shard_map/lv,bvne->blne/dot_general | solution.py:67
  10.4 0.4 copy.30
  10.8 0.5 broadcast.100
  11.3 2.2 %reduce.6 = bf16[256,512]{1,0:T(8,128)(2,1)S(1)} reduce(bf16[256,1,1,512]{3,2,1,0:T(2,128)(2,1)S(1)} %bitcast.95, bf16[]{:T(256)} %broadcast.100), dimensions={1,2}, to_apply=%bitcast.91.reduce_sub_computation | reduce | bytes 524290
  13.7 18.7 %all_to_all.23 = bf16[16,2,4096]{2,1,0:T(2,128)(2,1)S(1)} all-to-all(bf16[16,2,4096]{2,1,0:T(2,128)(2,1)S(1)} %reshape.122), channel_id=1, replica_groups=mesh['var'=16,'dp'=32] {'var'}, dimensions={0} | all-to-all | bytes 524288 | tf_op jit(solution)/shard_map/all_to_all | solution.py:68
  33.1 2.2 %fusion.26 = f32[256,2048]{1,0:T(8,128)} fusion(bf16[512,2048]{1,0:T(8,128)(2,1)S(1)} %copy-done, bf16[1,1,256,512]{3,2,1,0:T(8,128)(2,1)S(1)} %get-tuple-element.5, f32[512]{0:T(512)S(1)} %copy-done.3, f32[256]{0:T(256)S(1)} %add_rsqrt_fusion, f32[256]{0:T(256)S(1)} %broadcast_multiply_fusion.3), kind=kOutput, calls=%fused_computation.35 | convolution fusion | flops 537526272 | bytes 4460544 | tf_op jit(solution)/shard_map/dot_general | solution.py:27
  35.3 4.6 %fusion.43 = (f32[256]{0:T(256)S(1)}, f32[256]{0:T(256)S(1)}, f32[256,512]{1,0:T(8,128)S(1)}) fusion(f32[256]{0:T(256)S(1)} %add_rsqrt_fusion, f32[256]{0:T(256)S(1)} %broadcast_multiply_fusion.3, bf16[1,1,256,512]{3,2,1,0:T(8,128)(2,1)S(1)} %get-tuple-element.5, f32[512]{0:T(512)S(1)} %copy-done.3, bf16[512,2048]{1,0:T(8,128)(2,1)S(1)} %copy-done, ...), kind=kOutput, calls=%fused_computation.59 | convolution fusion | flops 1085144576 | bytes 7346176 | tf_op jit(solution)/shard_map/dot_general | solution.py:36
  39.9 1.0 %fusion.22 = bf16[256,512]{1,0:T(8,128)(2,1)} fusion(bf16[1,1,256,512]{3,2,1,0:T(8,128)(2,1)S(1)} %get-tuple-element.5, f32[256,512]{1,0:T(8,128)S(1)} %get-tuple-element.6, f32[256]{0:T(256)S(1)} %get-tuple-element.7, f32[256]{0:T(256)S(1)} %get-tuple-element.8, f32[256]{0:T(256)S(1)} %add_rsqrt_fusion, f32[256]{0:T(256)S(1)} %broadcast_multiply_fusion.3, ...), kind=kLoop, calls=%fused_computation.30 | loop fusion | flops 1310720 | bytes 1314816 | tf_op jit(solution)/shard_map/convert_element_type | solution.py:45
  40.9 3.8 %all-to-all-start.1 = ((bf16[1,16,16,512]{3,2,0,1:T(8,128)(2,1)}), bf16[1,16,16,512]{3,2,0,1:T(8,128)(2,1)S(1)}, u32[]{:S(2)}, u32[]{:S(2)}) async-start(bf16[1,16,16,512]{3,2,0,1:T(8,128)(2,1)} %bitcast.11), calls=%async_computation.1 | async-start | bytes 524288 | tf_op jit(solution)/shard_map/all_to_all | solution.py:70
  44.7 8.6 %all-to-all-done.1 = bf16[1,16,16,512]{3,2,0,1:T(8,128)(2,1)S(1)} async-done(((bf16[1,16,16,512]{3,2,0,1:T(8,128)(2,1)}), bf16[1,16,16,512]{3,2,0,1:T(8,128)(2,1)S(1)}, u32[]{:S(2)}, u32[]{:S(2)}) %all-to-all-start.1) | async-done | bytes 262176 | tf_op jit(solution)/shard_map/all_to_all | solution.py:70
  53.5 0.4 reshape.116
  53.9 1.6 %copy.29 = f32[4,16,32,16]{3,1,0,2:T(8,128)} copy(f32[4,16,32,16]{3,2,1,0:T(8,128)S(1)} %reshape.116) | data formatting | bytes 262144 | tf_op jit(solution)/shard_map/reshape | solution.py:77
  55.5 2.3 %reshape.124 = f32[32,1,1024]{2,1,0:T(1,128)} reshape(f32[32,4,16,16]{3,2,1,0:T(8,128)} %bitcast.92) | data formatting | bytes 262144
  57.8 18.4 %all-to-all-start.2 = ((f32[32,1,1024]{2,1,0:T(1,128)}), f32[32,1,1024]{2,1,0:T(1,128)S(1)}, u32[]{:S(2)}, u32[]{:S(2)}) async-start(f32[32,1,1024]{2,1,0:T(1,128)} %reshape.124), calls=%async_computation.2 | async-start | bytes 262144 | tf_op jit(solution)/shard_map/all_to_all | solution.py:78
  76.2 3.8 %fusion.7 = bf16[256,512]{1,0:T(8,128)(2,1)} fusion(bf16[2048,512]{1,0:T(8,128)(2,1)} %param.12, f32[256,2048]{1,0:T(8,128)} %fusion.26, bf16[1,1,256,512]{3,2,1,0:T(8,128)(2,1)S(1)} %get-tuple-element.5), kind=kOutput, calls=%fused_computation.13 | convolution fusion | flops 541982720 | bytes 4718592 | tf_op jit(solution)/shard_map/dot_general | solution.py:29
  79.9 11.9 %all-to-all-done.2 = f32[32,1,1024]{2,1,0:T(1,128)S(1)} async-done(((f32[32,1,1024]{2,1,0:T(1,128)}), f32[32,1,1024]{2,1,0:T(1,128)S(1)}, u32[]{:S(2)}, u32[]{:S(2)}) %all-to-all-start.2) | async-done | bytes 131104 | tf_op jit(solution)/shard_map/all_to_all | solution.py:78
  91.8 0.5 broadcast.101
  92.3 0.9 %reduce.7 = f32[32,1024]{1,0:T(8,128)S(1)} reduce(f32[32,1,1024]{2,1,0:T(1,128)S(1)} %all-to-all-done.2, f32[]{:T(128)} %broadcast.101), dimensions={1}, to_apply=%all_to_all.8.reduce_sub_computation | reduce | bytes 262148 | tf_op jit(solution)/shard_map/all_to_all | solution.py:78
  93.8 0.6 broadcast_multiply_fusion
  (24 shorter events, 1.7 us)
Async XLA Ops:
  0.6 32.5 %copy-start = (bf16[512,2048]{1,0:T(8,128)(2,1)S(1)}, bf16[512,2048]{1,0:T(8,128)(2,1)}, u32[]{:S(2)}) copy-start(bf16[512,2048]{1,0:T(8,128)(2,1)} %param.11) | copy-start | bytes 6291460
  0.6 4.2 %copy-start.2 = (bf16[4,16,512]{2,1,0:T(8,128)(2,1)S(1)}, bf16[4,16,512]{2,1,0:T(8,128)(2,1)}, u32[]{:S(2)}) copy-start(bf16[4,16,512]{2,1,0:T(8,128)(2,1)} %param.8) | copy-start | bytes 196612
  3.8 3.3 %copy-start.4 = (s32[4]{0:T(128)S(1)}, s32[4]{0:T(128)}, u32[]{:S(2)}) copy-start(s32[4]{0:T(128)} %param.9) | copy-start | bytes 52
  10.4 22.7 %copy-start.3 = (f32[512]{0:T(512)S(1)}, f32[512]{0:T(512)}, u32[]{:S(2)}) copy-start(f32[512]{0:T(512)} %param.10) | copy-start | bytes 6148
  33.1 2.2 %copy-start.1 = (bf16[1,16,16,512]{3,2,1,0:T(8,128)(2,1)S(1)}, bf16[1,16,16,512]{3,2,1,0:T(8,128)(2,1)}, u32[]{:S(2)}) copy-start(bf16[1,16,16,512]{3,2,1,0:T(8,128)(2,1)} %param.13) | copy-start | bytes 786436
  40.9 12.4 %all-to-all-start.1 = ((bf16[1,16,16,512]{3,2,0,1:T(8,128)(2,1)}), bf16[1,16,16,512]{3,2,0,1:T(8,128)(2,1)S(1)}, u32[]{:S(2)}, u32[]{:S(2)}) async-start(bf16[1,16,16,512]{3,2,0,1:T(8,128)(2,1)} %bitcast.11), calls=%async_computation.1 | async-start | bytes 524288 | tf_op jit(solution)/shard_map/all_to_all | solution.py:70
  57.8 34.1 %all-to-all-start.2 = ((f32[32,1,1024]{2,1,0:T(1,128)}), f32[32,1,1024]{2,1,0:T(1,128)S(1)}, u32[]{:S(2)}, u32[]{:S(2)}) async-start(f32[32,1,1024]{2,1,0:T(1,128)} %reshape.124), calls=%async_computation.2 | async-start | bytes 262144 | tf_op jit(solution)/shard_map/all_to_all | solution.py:78

commit v2 on v0

--- a/solution.py
+++ b/solution.py
@@ -54,25 +54,41 @@
     return (onehot * inv[:, None], inv[level] * weight)
 
 
+def patch_rows(fields):
+    batch, count_v, height, width = fields.shape
+    shaped = fields.reshape(batch, count_v, height // PATCH, PATCH, width // PATCH, PATCH)
+    return shaped.transpose(0, 2, 4, 1, 3, 5).reshape(
+        batch, height // PATCH * (width // PATCH), count_v * PATCH * PATCH
+    )
+
+
 def local(fields, kernels, level_map, norm_gain_vector, w_in, w_out, cotangent):
-    batch, var_local = (fields.shape[0], fields.shape[1])
-    patch_inputs = patches_of(fields)
-    tokens_all = patch_inputs.shape[2]
-    scale = float(batch * lax.axis_size("dp") * tokens_all) ** (-0.5)
+    var_local, patch_n, width = kernels.shape
+    parts = lax.axis_size("dp")
+    rows = patch_rows(fields)
+    batch, tokens_all = rows.shape[0], rows.shape[1]
+    scale = float(batch * parts * tokens_all) ** (-0.5)
     own_level = jnp.zeros((var_local,), jnp.int32)
-    own_assign, own_member = level_tables(own_level, level_map.astype(jnp.float32), 1)
-    patch_embeddings = jnp.einsum(
-        "bvnp,vpe->bvne", patch_inputs, kernels, preferred_element_type=jnp.float32
-    )
-    token_rows = jnp.einsum("lv,bvne->blne", own_assign, patch_embeddings).astype(jnp.bfloat16)
-    row_tokens = lax.all_to_all(token_rows, "var", split_axis=2, concat_axis=1, tiled=True)
+    _, own_member = level_tables(own_level, level_map.astype(jnp.float32), 1)
+    weighted = (kernels.astype(jnp.float32) * own_member[:, None, None]).reshape(-1, width)
+    token_rows = jnp.einsum(
+        "bnk,ke->bne",
+        rows.astype(jnp.float32),
+        weighted,
+        precision=lax.Precision.HIGHEST,
+        preferred_element_type=jnp.float32,
+    ).astype(jnp.bfloat16)
+    chunks = lax.axis_size("var")
+    token_rows = token_rows.reshape(batch, chunks, tokens_all // chunks, width)
+    row_tokens = lax.all_to_all(token_rows, "var", split_axis=1, concat_axis=1, tiled=True)
     block_out, token_gradient = block_pass(row_tokens, cotangent, norm_gain_vector, w_in, w_out)
-    dlevel = lax.all_to_all(token_gradient, "var", split_axis=1, concat_axis=2, tiled=True)
-    partial_grad = (
-        jnp.einsum("bvnp,bne->vpe", patch_inputs, dlevel[:, 0], preferred_element_type=jnp.float32)
-        * own_member[:, None, None]
-    )
-    kernel_grad = lax.psum_scatter(partial_grad, "dp", scatter_dimension=2, tiled=True) * scale
+    dlevel = lax.all_to_all(token_gradient, "var", split_axis=1, concat_axis=1, tiled=True)
+    dlevel = dlevel.reshape(batch, tokens_all, width)
+    partial_grad = jnp.einsum("bne,bnk->ek", dlevel, rows, preferred_element_type=jnp.float32)
+    pieces = partial_grad.reshape(parts, width // parts, var_local * patch_n)
+    gathered = lax.all_to_all(pieces, "dp", split_axis=0, concat_axis=0, tiled=True)
+    summed = jnp.sum(gathered, axis=0).T.reshape(var_local, patch_n, width // parts)
+    kernel_grad = summed * (own_member * scale)[:, None, None]
     return (block_out, kernel_grad)
 
 

time: 184 us -> 86.1 us (0.47)
  waiting for transfers between devices: 116 us -> 20.4 us
  starting transfers between devices: 3.79 us -> 22.2 us
  between operations: 14.9 us -> 1.48 us
  local copies, waits for them, and re-layouts: 9.68 us -> 5.96 us
  matrix products: 13.1 us -> 11.1 us
    unnamed x2 -> x0, waiting for transfers between devices: 108 us -> none
    all_to_all x1 -> x2, starting transfers between devices: 3.75 us -> 22.2 us  [the longest x1 18.4 us: local(): lax.all_to_all(pieces, 'dp', split_axis=0, concat_axis=0, tiled=True)]
    all_to_all x1 -> x2, waiting for transfers between devices: 8.55 us -> 20.4 us  [the longest x1 11.9 us: local(): lax.all_to_all(pieces, 'dp', split_axis=0, concat_axis=0, tiled=True)]
    unnamed x17 -> x10, local copies, waits for them, and re-layouts: 3.43 us -> 0.97 us
    unnamed x1 -> x0, other arithmetic: 2.27 us -> none
  transfers between devices with their start and end apart: 2 -> 2, of which waited for: 2 -> 2; matrix products, arithmetic and copies ran while one was open for 2% -> 5% of each run, Pallas kernels for 0% -> 0%
where the time goes in v2:
time: 86.1 us; the launch traced here: 85.1 us
  starting transfers between devices  22.2 us (26%)
  waiting for transfers between devices  20.4 us (24%)
  blocking collectives  18.7 us (22%)
  matrix products  11.1 us (13%)
  local copies, waits for them, and re-layouts  5.96 us (7%)
  other arithmetic  5.27 us (6%)
  between operations  1.48 us (2%)
    all_to_all x1, blocking collectives, local(): lax.all_to_all(token_rows, 'var', split_axis=1, concat_axis=1, tiled=True)  18.7 us
    all_to_all x1, starting transfers between devices, local(): lax.all_to_all(pieces, 'dp', split_axis=0, concat_axis=0, tiled=True)  18.4 us
    all_to_all x1, waiting for transfers between devices, local(): lax.all_to_all(pieces, 'dp', split_axis=0, concat_axis=0, tiled=True)  11.9 us
    all_to_all x1, waiting for transfers between devices, local(): lax.all_to_all(token_gradient, 'var', split_axis=1, concat_axis=1, tiled=...  8.49 us
    dot_general x1, matrix products, block_pass(): dnorm = jnp.dot(dpre, w_in.T, preferred_element_type=jnp.float32)  4.67 us
    all_to_all x1, starting transfers between devices, local(): lax.all_to_all(token_gradient, 'var', split_axis=1, concat_axis=1, tiled=...  3.75 us
    dot_general x1, matrix products, block_pass(): jnp.dot(hidden, w_out, preferred_element_type=jnp.float32)  3.74 us
    reshape x1, local copies, waits for them, and re-layouts, patch_rows(): fields.reshape(batch, count_v, height // PATCH, PATCH, width // PATCH, PA...  2.97 us
  transfers between devices with their start and end apart: 2, of which 2 were waited for; matrix products, arithmetic and copies ran while one was open for 5% of the time, Pallas kernels for 0%

profile of v2, /device:TPU:1, one launch (start us, length us, event | category | flops | bytes accessed | tf_op | source)
XLA Modules:
  0.0 85.1 jit_solution(11604320594139139812)
XLA Ops:
  0.7 1.4 %convert_reduce_fusion.1 = f32[]{:T(128)} fusion(s32[4]{0:T(128)} %param.9), kind=kLoop, calls=%fused_computation.31 | loop fusion | flops 7 | bytes 20 | tf_op jit(solution)/shard_map/reduce_sum | solution.py:53
  2.8 0.7 broadcast_multiply_fusion.4
  3.4 3.0 %reshape.98 = bf16[1,4,8,4,32,4]{5,4,3,2,1,0:T(8,128)(2,1)S(1)} reshape(bf16[1,4,32,128]{3,2,1,0:T(8,128)(2,1)} %param.7) | data formatting | bytes 65536 | tf_op jit(solution)/shard_map/reshape | solution.py:59
  6.4 0.9 %copy.14 = bf16[1,8,32,4,4,4]{2,1,5,4,3,0:T(8,128)(2,1)S(1)} copy(bf16[1,8,32,4,4,4]{5,2,4,1,3,0:T(8,128)(2,1)S(1)} %bitcast.51) | data formatting | bytes 65536 | tf_op jit(solution)/shard_map/transpose | solution.py:60
  7.3 0.1 reshape.99
  7.5 0.4 convolution_convert_fusion
  7.9 18.7 %all_to_all.15 = bf16[1,16,16,512]{3,2,0,1:T(8,128)(2,1)S(1)} all-to-all(bf16[1,16,16,512]{3,2,0,1:T(8,128)(2,1)S(1)} %bitcast.54), channel_id=1, replica_groups=mesh['var'=16,'dp'=32] {'var'}, dimensions={1} | all-to-all | bytes 524288 | tf_op jit(solution)/shard_map/all_to_all | solution.py:83
  26.9 0.2 multiply_reduce_fusion.1
  27.2 0.1 multiply_convert_fusion.2
  27.4 2.1 %fusion.26 = f32[256,2048]{1,0:T(8,128)} fusion(bf16[256,512]{1,0:T(8,128)(2,1)S(1)} %multiply_convert_fusion.2, bf16[512,2048]{1,0:T(8,128)(2,1)S(1)} %copy-done), kind=kOutput, calls=%fused_computation.45 | convolution fusion | flops 536870912 | bytes 4456448 | tf_op jit(solution)/shard_map/dot_general | solution.py:27
  29.5 4.7 %fusion.23 = (f32[256]{0:T(256)S(1)}, f32[256]{0:T(256)S(1)}, f32[256,512]{1,0:T(8,128)S(1)}) fusion(f32[256]{0:T(256)S(1)} %rsqrt.12, f32[256]{0:T(256)S(1)} %div.20, bf16[1,16,16,512]{3,2,0,1:T(8,128)(2,1)S(1)} %all_to_all.15, f32[512]{0:T(512)S(1)} %copy-done.3, bf16[512,2048]{1,0:T(8,128)(2,1)S(1)} %copy-done, f32[256,2048]{1,0:T(8,128)} %fusion.26, ...), kind=kOutput, calls=%fused_computation.43 | convolution fusion | flops 1085144576 | bytes 7346176 | tf_op jit(solution)/shard_map/dot_general | solution.py:36
  34.1 1.0 %add_convert_fusion = bf16[256,512]{1,0:T(8,128)(2,1)} fusion(f32[256,512]{1,0:T(8,128)S(1)} %get-tuple-element.6, bf16[1,16,16,512]{3,2,0,1:T(8,128)(2,1)S(1)} %all_to_all.15, f32[256]{0:T(256)S(1)} %get-tuple-element.7, f32[256]{0:T(256)S(1)} %get-tuple-element.8, f32[256]{0:T(256)S(1)} %rsqrt.12, f32[256]{0:T(256)S(1)} %div.20, ...), kind=kLoop, calls=%fused_computation.19 | loop fusion | flops 1310720 | bytes 1314816 | tf_op jit(solution)/shard_map/convert_element_type | solution.py:45
  35.1 3.8 %all-to-all-start.1 = ((bf16[1,16,16,512]{3,2,0,1:T(8,128)(2,1)}), bf16[1,16,16,512]{3,2,0,1:T(8,128)(2,1)S(1)}, u32[]{:S(2)}, u32[]{:S(2)}) async-start(bf16[1,16,16,512]{3,2,0,1:T(8,128)(2,1)} %bitcast.9), calls=%async_computation.1 | async-start | bytes 524288 | tf_op jit(solution)/shard_map/all_to_all | solution.py:85
  38.9 0.1 reshape.107
  39.0 8.5 %all-to-all-done.1 = bf16[1,16,16,512]{3,2,0,1:T(8,128)(2,1)S(1)} async-done(((bf16[1,16,16,512]{3,2,0,1:T(8,128)(2,1)}), bf16[1,16,16,512]{3,2,0,1:T(8,128)(2,1)S(1)}, u32[]{:S(2)}, u32[]{:S(2)}) %all-to-all-start.1) | async-done | bytes 262176 | tf_op jit(solution)/shard_map/all_to_all | solution.py:85
  47.5 0.1 copy.17
  47.6 0.2 fusion.27
  47.8 0.8 reshape.109
  48.6 18.4 %all-to-all-start.2 = ((f32[32,1,1024]{2,1,0:T(1,128)}), f32[32,1,1024]{2,1,0:T(1,128)S(1)}, u32[]{:S(2)}, u32[]{:S(2)}) async-start(f32[32,1,1024]{2,1,0:T(1,128)} %reshape.109), calls=%async_computation.2 | async-start | bytes 262144 | tf_op jit(solution)/shard_map/all_to_all | solution.py:89
  67.1 3.7 %fusion.7 = bf16[256,512]{1,0:T(8,128)(2,1)} fusion(bf16[2048,512]{1,0:T(8,128)(2,1)} %param.12, f32[256,2048]{1,0:T(8,128)} %fusion.26, bf16[256,512]{1,0:T(8,128)(2,1)S(1)} %bitcast.50), kind=kOutput, calls=%fused_computation.12 | convolution fusion | flops 541982720 | bytes 4718592 | tf_op jit(solution)/shard_map/dot_general | solution.py:29
  70.8 11.9 %all-to-all-done.2 = f32[32,1,1024]{2,1,0:T(1,128)S(1)} async-done(((f32[32,1,1024]{2,1,0:T(1,128)}), f32[32,1,1024]{2,1,0:T(1,128)S(1)}, u32[]{:S(2)}, u32[]{:S(2)}) %all-to-all-start.2) | async-done | bytes 131104 | tf_op jit(solution)/shard_map/all_to_all | solution.py:89
  82.7 0.5 broadcast.107
  83.2 1.0 %reduce.4 = f32[32,1024]{1,0:T(8,128)S(1)} reduce(f32[32,1,1024]{2,1,0:T(1,128)S(1)} %all-to-all-done.2, f32[]{:T(128)} %broadcast.107), dimensions={1}, to_apply=%all_to_all.11.reduce_sub_computation | reduce | bytes 262148 | tf_op jit(solution)/shard_map/all_to_all | solution.py:89
  84.4 0.7 broadcast_multiply_fusion
  (18 shorter events, 0.6 us)
Async XLA Ops:
  0.6 26.7 %copy-start = (bf16[512,2048]{1,0:T(8,128)(2,1)S(1)}, bf16[512,2048]{1,0:T(8,128)(2,1)}, u32[]{:S(2)}) copy-start(bf16[512,2048]{1,0:T(8,128)(2,1)} %param.11) | copy-start | bytes 6291460
  0.6 6.8 %copy-start.2 = (bf16[4,16,512]{2,1,0:T(8,128)(2,1)S(1)}, bf16[4,16,512]{2,1,0:T(8,128)(2,1)}, u32[]{:S(2)}) copy-start(bf16[4,16,512]{2,1,0:T(8,128)(2,1)} %param.8) | copy-start | bytes 196612
  0.7 26.5 %copy-start.3 = (f32[512]{0:T(512)S(1)}, f32[512]{0:T(512)}, u32[]{:S(2)}) copy-start(f32[512]{0:T(512)} %param.10) | copy-start | bytes 6148
  27.3 2.1 %copy-start.1 = (bf16[1,16,16,512]{3,2,1,0:T(8,128)(2,1)S(1)}, bf16[1,16,16,512]{3,2,1,0:T(8,128)(2,1)}, u32[]{:S(2)}) copy-start(bf16[1,16,16,512]{3,2,1,0:T(8,128)(2,1)} %param.13) | copy-start | bytes 786436
  35.1 12.4 %all-to-all-start.1 = ((bf16[1,16,16,512]{3,2,0,1:T(8,128)(2,1)}), bf16[1,16,16,512]{3,2,0,1:T(8,128)(2,1)S(1)}, u32[]{:S(2)}, u32[]{:S(2)}) async-start(bf16[1,16,16,512]{3,2,0,1:T(8,128)(2,1)} %bitcast.9), calls=%async_computation.1 | async-start | bytes 524288 | tf_op jit(solution)/shard_map/all_to_all | solution.py:85
  48.6 34.1 %all-to-all-start.2 = ((f32[32,1,1024]{2,1,0:T(1,128)}), f32[32,1,1024]{2,1,0:T(1,128)S(1)}, u32[]{:S(2)}, u32[]{:S(2)}) async-start(f32[32,1,1024]{2,1,0:T(1,128)} %reshape.109), calls=%async_computation.2 | async-start | bytes 262144 | tf_op jit(solution)/shard_map/all_to_all | solution.py:89

commit v3 on v2

--- a/solution.py
+++ b/solution.py
@@ -85,9 +85,9 @@
     dlevel = lax.all_to_all(token_gradient, "var", split_axis=1, concat_axis=1, tiled=True)
     dlevel = dlevel.reshape(batch, tokens_all, width)
     partial_grad = jnp.einsum("bne,bnk->ek", dlevel, rows, preferred_element_type=jnp.float32)
-    pieces = partial_grad.reshape(parts, width // parts, var_local * patch_n)
+    pieces = partial_grad.reshape(parts, width // parts, var_local * patch_n).astype(jnp.bfloat16)
     gathered = lax.all_to_all(pieces, "dp", split_axis=0, concat_axis=0, tiled=True)
-    summed = jnp.sum(gathered, axis=0).T.reshape(var_local, patch_n, width // parts)
+    summed = jnp.sum(gathered.astype(jnp.float32), axis=0).T.reshape(var_local, patch_n, width // parts)
     kernel_grad = summed * (own_member * scale)[:, None, None]
     return (block_out, kernel_grad)
 

time: 86.1 us -> 82.9 us (0.963)
  waiting for transfers between devices: 20.4 us -> 19.3 us
  other arithmetic: 5.27 us -> 4.33 us
    all_to_all x1, waiting for transfers between devices: 11.9 us -> 10.8 us  [local(): lax.all_to_all(pieces, 'dp', split_axis=0, concat_axis=0, tiled=True)]
    all_to_all x1 -> x0, other arithmetic: 0.95 us -> none  [local(): lax.all_to_all(pieces, 'dp', split_axis=0, concat_axis=0, tiled=True)]
where the time goes in v3:
time: 82.9 us; the launch traced here: 82.5 us
  starting transfers between devices  22.1 us (27%)
  waiting for transfers between devices  19.3 us (23%)
  blocking collectives  18.7 us (23%)
  matrix products  11.1 us (13%)
  local copies, waits for them, and re-layouts  5.43 us (7%)
  other arithmetic  4.33 us (5%)
  between operations  1.48 us (2%)
    all_to_all x1, blocking collectives, local(): lax.all_to_all(token_rows, 'var', split_axis=1, concat_axis=1, tiled=True)  18.7 us
    all_to_all x1, starting transfers between devices, local(): lax.all_to_all(pieces, 'dp', split_axis=0, concat_axis=0, tiled=True)  18.4 us
    all_to_all x1, waiting for transfers between devices, local(): lax.all_to_all(pieces, 'dp', split_axis=0, concat_axis=0, tiled=True)  10.8 us
    all_to_all x1, waiting for transfers between devices, local(): lax.all_to_all(token_gradient, 'var', split_axis=1, concat_axis=1, tiled=...  8.49 us
    dot_general x1, matrix products, block_pass(): dnorm = jnp.dot(dpre, w_in.T, preferred_element_type=jnp.float32)  4.64 us
    all_to_all x1, starting transfers between devices, local(): lax.all_to_all(token_gradient, 'var', split_axis=1, concat_axis=1, tiled=...  3.75 us
    dot_general x1, matrix products, block_pass(): jnp.dot(hidden, w_out, preferred_element_type=jnp.float32)  3.74 us
    reshape x1, local copies, waits for them, and re-layouts, patch_rows(): fields.reshape(batch, count_v, height // PATCH, PATCH, width // PATCH, PA...  2.99 us
  transfers between devices with their start and end apart: 2, of which 2 were waited for; matrix products, arithmetic and copies ran while one was open for 5% of the time, Pallas kernels for 0%

profile of v3, /device:TPU:1, one launch (start us, length us, event | category | flops | bytes accessed | tf_op | source)
XLA Modules:
  0.0 82.5 jit_solution(4569863996934350071)
XLA Ops:
  0.7 1.4 %convert_reduce_fusion.2 = f32[]{:T(128)} fusion(s32[4]{0:T(128)} %param.9), kind=kLoop, calls=%fused_computation.33 | loop fusion | flops 7 | bytes 20 | tf_op jit(solution)/shard_map/reduce_sum | solution.py:53
  2.8 0.7 broadcast_multiply_fusion.4
  3.4 3.0 %reshape.98 = bf16[1,4,8,4,32,4]{5,4,3,2,1,0:T(8,128)(2,1)S(1)} reshape(bf16[1,4,32,128]{3,2,1,0:T(8,128)(2,1)} %param.7) | data formatting | bytes 65536 | tf_op jit(solution)/shard_map/reshape | solution.py:59
  6.4 0.9 %copy.14 = bf16[1,8,32,4,4,4]{2,1,5,4,3,0:T(8,128)(2,1)S(1)} copy(bf16[1,8,32,4,4,4]{5,2,4,1,3,0:T(8,128)(2,1)S(1)} %bitcast.51) | data formatting | bytes 65536 | tf_op jit(solution)/shard_map/transpose | solution.py:60
  7.3 0.1 reshape.99
  7.5 0.4 convolution_convert_fusion
  8.0 18.7 %all_to_all.15 = bf16[1,16,16,512]{3,2,0,1:T(8,128)(2,1)S(1)} all-to-all(bf16[1,16,16,512]{3,2,0,1:T(8,128)(2,1)S(1)} %bitcast.53), channel_id=1, replica_groups=mesh['var'=16,'dp'=32] {'var'}, dimensions={1} | all-to-all | bytes 524288 | tf_op jit(solution)/shard_map/all_to_all | solution.py:83
  26.7 0.1 convert_reduce_fusion
  26.9 0.2 multiply_reduce_fusion.1
  27.2 0.1 multiply_convert_fusion.2
  27.4 2.1 %fusion.26 = f32[256,2048]{1,0:T(8,128)} fusion(bf16[256,512]{1,0:T(8,128)(2,1)S(1)} %multiply_convert_fusion.2, bf16[512,2048]{1,0:T(8,128)(2,1)S(1)} %copy-done), kind=kOutput, calls=%fused_computation.47 | convolution fusion | flops 536870912 | bytes 4456448 | tf_op jit(solution)/shard_map/dot_general | solution.py:27
  29.5 4.6 %fusion.23 = (f32[256]{0:T(256)S(1)}, f32[256]{0:T(256)S(1)}, f32[256,512]{1,0:T(8,128)S(1)}) fusion(f32[256]{0:T(256)S(1)} %rsqrt.12, f32[256]{0:T(256)S(1)} %div.20, bf16[1,16,16,512]{3,2,0,1:T(8,128)(2,1)S(1)} %all_to_all.15, f32[512]{0:T(512)S(1)} %copy-done.3, bf16[512,2048]{1,0:T(8,128)(2,1)S(1)} %copy-done, f32[256,2048]{1,0:T(8,128)} %fusion.26, ...), kind=kOutput, calls=%fused_computation.45 | convolution fusion | flops 1085144576 | bytes 7346176 | tf_op jit(solution)/shard_map/dot_general | solution.py:36
  34.1 1.0 %add_convert_fusion = bf16[256,512]{1,0:T(8,128)(2,1)} fusion(f32[256,512]{1,0:T(8,128)S(1)} %get-tuple-element.6, bf16[1,16,16,512]{3,2,0,1:T(8,128)(2,1)S(1)} %all_to_all.15, f32[256]{0:T(256)S(1)} %get-tuple-element.7, f32[256]{0:T(256)S(1)} %get-tuple-element.8, f32[256]{0:T(256)S(1)} %rsqrt.12, f32[256]{0:T(256)S(1)} %div.20, ...), kind=kLoop, calls=%fused_computation.20 | loop fusion | flops 1310720 | bytes 1314816 | tf_op jit(solution)/shard_map/convert_element_type | solution.py:45
  35.1 3.8 %all-to-all-start.1 = ((bf16[1,16,16,512]{3,2,0,1:T(8,128)(2,1)}), bf16[1,16,16,512]{3,2,0,1:T(8,128)(2,1)S(1)}, u32[]{:S(2)}, u32[]{:S(2)}) async-start(bf16[1,16,16,512]{3,2,0,1:T(8,128)(2,1)} %bitcast.9), calls=%async_computation.1 | async-start | bytes 524288 | tf_op jit(solution)/shard_map/all_to_all | solution.py:85
  38.9 0.1 reshape.107
  39.0 8.5 %all-to-all-done.1 = bf16[1,16,16,512]{3,2,0,1:T(8,128)(2,1)S(1)} async-done(((bf16[1,16,16,512]{3,2,0,1:T(8,128)(2,1)}), bf16[1,16,16,512]{3,2,0,1:T(8,128)(2,1)S(1)}, u32[]{:S(2)}, u32[]{:S(2)}) %all-to-all-start.1) | async-done | bytes 262176 | tf_op jit(solution)/shard_map/all_to_all | solution.py:85
  47.5 0.1 copy.17
  47.6 0.2 convolution_convert_fusion.1
  47.8 0.8 reshape.109
  48.6 18.4 %all-to-all-start.2 = ((bf16[32,2,512]{2,1,0:T(2,128)(2,1)}), bf16[32,2,512]{2,1,0:T(2,128)(2,1)S(1)}, u32[]{:S(2)}, u32[]{:S(2)}) async-start(bf16[32,2,512]{2,1,0:T(2,128)(2,1)} %reshape.109), calls=%async_computation.2 | async-start | bytes 131072 | tf_op jit(solution)/shard_map/all_to_all | solution.py:89
  67.0 3.7 %fusion.7 = bf16[256,512]{1,0:T(8,128)(2,1)} fusion(bf16[2048,512]{1,0:T(8,128)(2,1)} %param.12, f32[256,2048]{1,0:T(8,128)} %fusion.26, bf16[256,512]{1,0:T(8,128)(2,1)S(1)} %bitcast.50), kind=kOutput, calls=%fused_computation.12 | convolution fusion | flops 541982720 | bytes 4718592 | tf_op jit(solution)/shard_map/dot_general | solution.py:29
  70.7 10.8 %all-to-all-done.2 = bf16[32,2,512]{2,1,0:T(2,128)(2,1)S(1)} async-done(((bf16[32,2,512]{2,1,0:T(2,128)(2,1)}), bf16[32,2,512]{2,1,0:T(2,128)(2,1)S(1)}, u32[]{:S(2)}, u32[]{:S(2)}) %all-to-all-start.2) | async-done | bytes 65568 | tf_op jit(solution)/shard_map/all_to_all | solution.py:89
  81.5 0.1 reshape.110
  81.8 0.7 broadcast_multiply_fusion
  (16 shorter events, 0.4 us)
Async XLA Ops:
  0.6 26.7 %copy-start = (bf16[512,2048]{1,0:T(8,128)(2,1)S(1)}, bf16[512,2048]{1,0:T(8,128)(2,1)}, u32[]{:S(2)}) copy-start(bf16[512,2048]{1,0:T(8,128)(2,1)} %param.11) | copy-start | bytes 6291460
  0.6 6.8 %copy-start.2 = (bf16[4,16,512]{2,1,0:T(8,128)(2,1)S(1)}, bf16[4,16,512]{2,1,0:T(8,128)(2,1)}, u32[]{:S(2)}) copy-start(bf16[4,16,512]{2,1,0:T(8,128)(2,1)} %param.8) | copy-start | bytes 196612
  0.7 26.5 %copy-start.3 = (f32[512]{0:T(512)S(1)}, f32[512]{0:T(512)}, u32[]{:S(2)}) copy-start(f32[512]{0:T(512)} %param.10) | copy-start | bytes 6148
  27.4 2.1 %copy-start.1 = (bf16[1,16,16,512]{3,2,1,0:T(8,128)(2,1)S(1)}, bf16[1,16,16,512]{3,2,1,0:T(8,128)(2,1)}, u32[]{:S(2)}) copy-start(bf16[1,16,16,512]{3,2,1,0:T(8,128)(2,1)} %param.13) | copy-start | bytes 786436
  35.1 12.4 %all-to-all-start.1 = ((bf16[1,16,16,512]{3,2,0,1:T(8,128)(2,1)}), bf16[1,16,16,512]{3,2,0,1:T(8,128)(2,1)S(1)}, u32[]{:S(2)}, u32[]{:S(2)}) async-start(bf16[1,16,16,512]{3,2,0,1:T(8,128)(2,1)} %bitcast.9), calls=%async_computation.1 | async-start | bytes 524288 | tf_op jit(solution)/shard_map/all_to_all | solution.py:85
  48.6 33.0 %all-to-all-start.2 = ((bf16[32,2,512]{2,1,0:T(2,128)(2,1)}), bf16[32,2,512]{2,1,0:T(2,128)(2,1)S(1)}, u32[]{:S(2)}, u32[]{:S(2)}) async-start(bf16[32,2,512]{2,1,0:T(2,128)(2,1)} %reshape.109), calls=%async_computation.2 | async-start | bytes 131072 | tf_op jit(solution)/shard_map/all_to_all | solution.py:89

commit v4 on v3

--- a/solution.py
+++ b/solution.py
@@ -30,7 +30,7 @@
         jnp.bfloat16
     )
     gradient_rows = grads.reshape(-1, width)
-    dhid = jnp.dot(gradient_rows, w_out.T, preferred_element_type=jnp.float32)
+    dhid = lax.optimization_barrier(jnp.dot(gradient_rows, w_out.T, preferred_element_type=jnp.float32))
     gelu_back = jax.vjp(lambda value: jax.nn.gelu(value, approximate=True), pre)[1]
     dpre = gelu_back(dhid)[0].astype(jnp.bfloat16)
     dnorm = jnp.dot(dpre, w_in.T, preferred_element_type=jnp.float32)

time: 82.9 us -> 79.2 us (0.955)
  blocking collectives: 18.7 us -> 0 us
  starting transfers between devices: 22.1 us -> 31.4 us
  waiting for transfers between devices: 19.3 us -> 25.2 us
  other arithmetic: 4.33 us -> 2.86 us
  local copies, waits for them, and re-layouts: 5.43 us -> 6.44 us
    all_to_all x1 -> x0, blocking collectives: 18.7 us -> none  [local(): lax.all_to_all(token_rows, 'var', split_axis=1, concat_axis=1, tiled=True)]
    all_to_all x0 -> x1, starting transfers between devices: none -> 9 us  [local(): lax.all_to_all(token_rows, 'var', split_axis=1, concat_axis=1, tiled=True)]
    all_to_all x0 -> x1, waiting for transfers between devices: none -> 5.87 us  [local(): lax.all_to_all(token_rows, 'var', split_axis=1, concat_axis=1, tiled=True)]
    dot_general x0 -> x1, matrix products: none -> 3.79 us  [block_pass(): jnp.dot(gradient_rows, w_out.T, preferred_element_type=jnp.float32)]
    dot_general x1, matrix products: 4.64 us -> 1.78 us  [block_pass(): dnorm = jnp.dot(dpre, w_in.T, preferred_element_type=jnp.float32)]
    dot_general x1, matrix products: 2.1 us -> 0.71 us  [block_pass(): pre = jnp.dot(normalized_rows, w_in, preferred_element_type=jnp.float32)]
    unnamed x10 -> x16, local copies, waits for them, and re-layouts: 0.93 us -> 1.8 us
  transfers between devices with their start and end apart: 2 -> 3, of which waited for: 2 -> 3; matrix products, arithmetic and copies ran while one was open for 5% -> 10% of each run, Pallas kernels for 0% -> 0%
where the time goes in v4:
time: 79.2 us; the launch traced here: 78.7 us
  starting transfers between devices  31.4 us (40%)
  waiting for transfers between devices  25.2 us (32%)
  matrix products  11.3 us (14%)
  local copies, waits for them, and re-layouts  6.44 us (8%)
  other arithmetic  2.86 us (4%)
  between operations  1.52 us (2%)
    all_to_all x1, starting transfers between devices, local(): lax.all_to_all(pieces, 'dp', split_axis=0, concat_axis=0, tiled=True)  18.5 us
    all_to_all x1, waiting for transfers between devices, local(): lax.all_to_all(pieces, 'dp', split_axis=0, concat_axis=0, tiled=True)  10.8 us
    all_to_all x1, starting transfers between devices, local(): lax.all_to_all(token_rows, 'var', split_axis=1, concat_axis=1, tiled=True)  9 us
    all_to_all x1, waiting for transfers between devices, local(): lax.all_to_all(token_gradient, 'var', split_axis=1, concat_axis=1, tiled=...  8.49 us
    all_to_all x1, waiting for transfers between devices, local(): lax.all_to_all(token_rows, 'var', split_axis=1, concat_axis=1, tiled=True)  5.87 us
    all_to_all x1, starting transfers between devices, local(): lax.all_to_all(token_gradient, 'var', split_axis=1, concat_axis=1, tiled=...  3.93 us
    dot_general x1, matrix products, block_pass(): jnp.dot(gradient_rows, w_out.T, preferred_element_type=jnp.float32)  3.79 us
    dot_general x1, matrix products, block_pass(): jnp.dot(hidden, w_out, preferred_element_type=jnp.float32)  3.74 us
  transfers between devices with their start and end apart: 3, of which 3 were waited for; matrix products, arithmetic and copies ran while one was open for 10% of the time, Pallas kernels for 0%

profile of v4, /device:TPU:1, one launch (start us, length us, event | category | flops | bytes accessed | tf_op | source)
XLA Modules:
  0.0 78.7 jit_solution(5778972837062813620)
XLA Ops:
  0.7 3.1 %reshape.98 = bf16[1,4,8,4,32,4]{5,4,3,2,1,0:T(8,128)(2,1)S(1)} reshape(bf16[1,4,32,128]{3,2,1,0:T(8,128)(2,1)} %param.7) | data formatting | bytes 65536 | tf_op jit(solution)/shard_map/reshape | solution.py:59
  3.8 0.9 %copy.14 = bf16[1,8,32,4,4,4]{2,1,5,4,3,0:T(8,128)(2,1)S(1)} copy(bf16[1,8,32,4,4,4]{5,2,4,1,3,0:T(8,128)(2,1)S(1)} %bitcast.51) | data formatting | bytes 65536 | tf_op jit(solution)/shard_map/transpose | solution.py:60
  4.7 0.1 reshape.99
  4.8 0.6 convert_reduce_fusion.2
  6.2 1.1 %convolution_convert_fusion = bf16[512,256]{0,1:T(8,128)(2,1)} fusion(f32[64,512]{1,0:T(8,128)S(1)} %bitcast.55, bf16[256,64]{0,1:T(8,128)(2,1)S(1)} %reshape.99), kind=kOutput, calls=%fused_computation.13 | convolution fusion | flops 100794368 | bytes 425984 | tf_op jit(solution)/shard_map/bnk,ke->bne/dot_general | solution.py:74
  7.3 9.0 %all-to-all-start = ((bf16[1,16,16,512]{3,2,0,1:T(8,128)(2,1)}), bf16[1,16,16,512]{3,2,0,1:T(8,128)(2,1)S(1)}, u32[]{:S(2)}, u32[]{:S(2)}) async-start(bf16[1,16,16,512]{3,2,0,1:T(8,128)(2,1)} %bitcast.4), calls=%async_computation | async-start | bytes 524288 | tf_op jit(solution)/shard_map/all_to_all | solution.py:83
  16.4 3.8 %fusion.25 = f32[256,2048]{1,0:T(8,128)} fusion(bf16[256,512]{1,0:T(8,128)(2,1)} %bitcast.52, bf16[2048,512]{1,0:T(8,128)(2,1)} %param.12), kind=kOutput, calls=%fused_computation.47 | convolution fusion | flops 536870912 | bytes 4456448 | tf_op jit(solution)/shard_map/dot_general | solution.py:33
  20.2 5.9 %all-to-all-done = bf16[1,16,16,512]{3,2,0,1:T(8,128)(2,1)S(1)} async-done(((bf16[1,16,16,512]{3,2,0,1:T(8,128)(2,1)}), bf16[1,16,16,512]{3,2,0,1:T(8,128)(2,1)S(1)}, u32[]{:S(2)}, u32[]{:S(2)}) %all-to-all-start) | async-done | bytes 262176 | tf_op jit(solution)/shard_map/all_to_all | solution.py:83
  26.2 0.2 multiply_reduce_fusion.1
  26.5 0.1 multiply_convert_fusion.2
  26.7 0.7 fusion.24
  27.4 0.9 %copy-done.2 = f32[256,2048]{1,0:T(8,128)S(1)} copy-done((f32[256,2048]{1,0:T(8,128)S(1)}, f32[256,2048]{1,0:T(8,128)}, u32[]{:S(2)}) %copy-start.2) | copy-done | bytes 2097176
  28.3 1.8 %fusion.23 = (f32[256]{0:T(256)S(1)}, f32[256]{0:T(256)S(1)}, f32[256,512]{1,0:T(8,128)S(1)}) fusion(f32[256]{0:T(256)S(1)} %rsqrt.12, f32[256]{0:T(256)S(1)} %div.20, bf16[1,16,16,512]{3,2,0,1:T(8,128)(2,1)S(1)} %all-to-all-done, f32[512]{0:T(512)S(1)} %copy-done.5, bf16[512,2048]{1,0:T(8,128)(2,1)S(1)} %copy-done, f32[256,2048]{1,0:T(8,128)S(1)} %fusion.24, ...), kind=kOutput, calls=%fused_computation.45 | convolution fusion | flops 548273664 | bytes 7084032 | tf_op jit(solution)/shard_map/dot_general | solution.py:36
  30.1 1.0 %add_convert_fusion = bf16[256,512]{1,0:T(8,128)(2,1)} fusion(f32[256,512]{1,0:T(8,128)S(1)} %get-tuple-element.6, bf16[1,16,16,512]{3,2,0,1:T(8,128)(2,1)S(1)} %all-to-all-done, f32[256]{0:T(256)S(1)} %get-tuple-element.7, f32[256]{0:T(256)S(1)} %get-tuple-element.8, f32[256]{0:T(256)S(1)} %rsqrt.12, f32[256]{0:T(256)S(1)} %div.20, ...), kind=kLoop, calls=%fused_computation.20 | loop fusion | flops 1310720 | bytes 1314816 | tf_op jit(solution)/shard_map/convert_element_type | solution.py:45
  31.1 3.9 %all-to-all-start.1 = ((bf16[1,16,16,512]{3,2,0,1:T(8,128)(2,1)}), bf16[1,16,16,512]{3,2,0,1:T(8,128)(2,1)S(1)}, u32[]{:S(2)}, u32[]{:S(2)}) async-start(bf16[1,16,16,512]{3,2,0,1:T(8,128)(2,1)} %bitcast.9), calls=%async_computation.1 | async-start | bytes 524288 | tf_op jit(solution)/shard_map/all_to_all | solution.py:85
  35.1 8.5 %all-to-all-done.1 = bf16[1,16,16,512]{3,2,0,1:T(8,128)(2,1)S(1)} async-done(((bf16[1,16,16,512]{3,2,0,1:T(8,128)(2,1)}), bf16[1,16,16,512]{3,2,0,1:T(8,128)(2,1)S(1)}, u32[]{:S(2)}, u32[]{:S(2)}) %all-to-all-start.1) | async-done | bytes 262176 | tf_op jit(solution)/shard_map/all_to_all | solution.py:85
  43.6 0.1 copy.17
  43.8 0.2 convolution_convert_fusion.1
  44.0 0.8 reshape.109
  44.7 18.5 %all-to-all-start.2 = ((bf16[32,2,512]{2,1,0:T(2,128)(2,1)}), bf16[32,2,512]{2,1,0:T(2,128)(2,1)S(1)}, u32[]{:S(2)}, u32[]{:S(2)}) async-start(bf16[32,2,512]{2,1,0:T(2,128)(2,1)} %reshape.109), calls=%async_computation.2 | async-start | bytes 131072 | tf_op jit(solution)/shard_map/all_to_all | solution.py:89
  63.2 3.7 %fusion.7 = bf16[256,512]{1,0:T(8,128)(2,1)} fusion(bf16[2048,512]{1,0:T(8,128)(2,1)} %param.12, f32[256,2048]{1,0:T(8,128)} %copy-done.1, bf16[256,512]{1,0:T(8,128)(2,1)S(1)} %bitcast.50), kind=kOutput, calls=%fused_computation.12 | convolution fusion | flops 541982720 | bytes 4718592 | tf_op jit(solution)/shard_map/dot_general | solution.py:29
  67.0 10.8 %all-to-all-done.2 = bf16[32,2,512]{2,1,0:T(2,128)(2,1)S(1)} async-done(((bf16[32,2,512]{2,1,0:T(2,128)(2,1)}), bf16[32,2,512]{2,1,0:T(2,128)(2,1)S(1)}, u32[]{:S(2)}, u32[]{:S(2)}) %all-to-all-start.2) | async-done | bytes 65568 | tf_op jit(solution)/shard_map/all_to_all | solution.py:89
  77.8 0.1 reshape.110
  78.1 0.7 broadcast_multiply_fusion
  (24 shorter events, 0.7 us)
Async XLA Ops:
  0.6 26.1 %copy-start = (bf16[512,2048]{1,0:T(8,128)(2,1)S(1)}, bf16[512,2048]{1,0:T(8,128)(2,1)}, u32[]{:S(2)}) copy-start(bf16[512,2048]{1,0:T(8,128)(2,1)} %param.11) | copy-start | bytes 6291460
  0.6 4.2 %copy-start.6 = (s32[4]{0:T(128)S(1)}, s32[4]{0:T(128)}, u32[]{:S(2)}) copy-start(s32[4]{0:T(128)} %param.9) | copy-start | bytes 52
  0.7 5.5 %copy-start.4 = (bf16[4,16,512]{2,1,0:T(8,128)(2,1)S(1)}, bf16[4,16,512]{2,1,0:T(8,128)(2,1)}, u32[]{:S(2)}) copy-start(bf16[4,16,512]{2,1,0:T(8,128)(2,1)} %param.8) | copy-start | bytes 196612
  7.3 18.7 %all-to-all-start = ((bf16[1,16,16,512]{3,2,0,1:T(8,128)(2,1)}), bf16[1,16,16,512]{3,2,0,1:T(8,128)(2,1)S(1)}, u32[]{:S(2)}, u32[]{:S(2)}) async-start(bf16[1,16,16,512]{3,2,0,1:T(8,128)(2,1)} %bitcast.4), calls=%async_computation | async-start | bytes 524288 | tf_op jit(solution)/shard_map/all_to_all | solution.py:83
  16.4 10.2 %copy-start.5 = (f32[512]{0:T(512)S(1)}, f32[512]{0:T(512)}, u32[]{:S(2)}) copy-start(f32[512]{0:T(512)} %param.10) | copy-start | bytes 6148
  26.7 1.6 %copy-start.2 = (f32[256,2048]{1,0:T(8,128)S(1)}, f32[256,2048]{1,0:T(8,128)}, u32[]{:S(2)}) copy-start(f32[256,2048]{1,0:T(8,128)} %fusion.25) | copy-start | bytes 6291460
  28.3 1.8 %copy-start.1 = (f32[256,2048]{1,0:T(8,128)}, f32[256,2048]{1,0:T(8,128)S(1)}, u32[]{:S(2)}) copy-start(f32[256,2048]{1,0:T(8,128)S(1)} %fusion.24) | copy-start | bytes 6291460
  28.3 1.8 %copy-start.3 = (bf16[1,16,16,512]{3,2,1,0:T(8,128)(2,1)S(1)}, bf16[1,16,16,512]{3,2,1,0:T(8,128)(2,1)}, u32[]{:S(2)}) copy-start(bf16[1,16,16,512]{3,2,1,0:T(8,128)(2,1)} %param.13) | copy-start | bytes 786436
  31.1 12.6 %all-to-all-start.1 = ((bf16[1,16,16,512]{3,2,0,1:T(8,128)(2,1)}), bf16[1,16,16,512]{3,2,0,1:T(8,128)(2,1)S(1)}, u32[]{:S(2)}, u32[]{:S(2)}) async-start(bf16[1,16,16,512]{3,2,0,1:T(8,128)(2,1)} %bitcast.9), calls=%async_computation.1 | async-start | bytes 524288 | tf_op jit(solution)/shard_map/all_to_all | solution.py:85
  44.7 33.0 %all-to-all-start.2 = ((bf16[32,2,512]{2,1,0:T(2,128)(2,1)}), bf16[32,2,512]{2,1,0:T(2,128)(2,1)S(1)}, u32[]{:S(2)}, u32[]{:S(2)}) async-start(bf16[32,2,512]{2,1,0:T(2,128)(2,1)} %reshape.109), calls=%async_computation.2 | async-start | bytes 131072 | tf_op jit(solution)/shard_map/all_to_all | solution.py:89

commit v5 on v4

--- a/solution.py
+++ b/solution.py
@@ -56,10 +56,10 @@
 
 def patch_rows(fields):
     batch, count_v, height, width = fields.shape
-    shaped = fields.reshape(batch, count_v, height // PATCH, PATCH, width // PATCH, PATCH)
-    return shaped.transpose(0, 2, 4, 1, 3, 5).reshape(
-        batch, height // PATCH * (width // PATCH), count_v * PATCH * PATCH
-    )
+    shaped = fields.reshape(batch, count_v, height // PATCH, PATCH, width)
+    shaped = shaped.transpose(0, 2, 1, 3, 4).reshape(batch, height // PATCH, count_v * PATCH, width)
+    flipped = jnp.swapaxes(shaped, -1, -2)
+    return flipped.reshape(batch, height // PATCH * (width // PATCH), PATCH * count_v * PATCH)
 
 
 def local(fields, kernels, level_map, norm_gain_vector, w_in, w_out, cotangent):
@@ -70,7 +70,8 @@
     scale = float(batch * parts * tokens_all) ** (-0.5)
     own_level = jnp.zeros((var_local,), jnp.int32)
     _, own_member = level_tables(own_level, level_map.astype(jnp.float32), 1)
-    weighted = (kernels.astype(jnp.float32) * own_member[:, None, None]).reshape(-1, width)
+    weighted = (kernels.astype(jnp.float32) * own_member[:, None, None]).reshape(var_local, PATCH, PATCH, width)
+    weighted = weighted.transpose(2, 0, 1, 3).reshape(-1, width)
     token_rows = jnp.einsum(
         "bnk,ke->bne",
         rows.astype(jnp.float32),
@@ -87,7 +88,8 @@
     partial_grad = jnp.einsum("bne,bnk->ek", dlevel, rows, preferred_element_type=jnp.float32)
     pieces = partial_grad.reshape(parts, width // parts, var_local * patch_n).astype(jnp.bfloat16)
     gathered = lax.all_to_all(pieces, "dp", split_axis=0, concat_axis=0, tiled=True)
-    summed = jnp.sum(gathered.astype(jnp.float32), axis=0).T.reshape(var_local, patch_n, width // parts)
+    summed = jnp.sum(gathered.astype(jnp.float32), axis=0).T.reshape(PATCH, var_local, PATCH, width // parts)
+    summed = summed.transpose(1, 2, 0, 3).reshape(var_local, patch_n, width // parts)
     kernel_grad = summed * (own_member * scale)[:, None, None]
     return (block_out, kernel_grad)
 

time: 79.2 us -> 77.7 us (0.981)
  blocking collectives: 0 us -> 13.4 us
  waiting for transfers between devices: 25.2 us -> 16.8 us
  starting transfers between devices: 31.4 us -> 26.4 us
  local copies, waits for them, and re-layouts: 6.44 us -> 3.44 us
  other arithmetic: 2.86 us -> 4.46 us
    all_to_all x0 -> x1, blocking collectives: none -> 13.4 us  [local(): lax.all_to_all(token_gradient, 'var', split_axis=1, concat_axis=1, tiled=...]
    all_to_all x1 -> x0, waiting for transfers between devices: 8.49 us -> none  [local(): lax.all_to_all(token_gradient, 'var', split_axis=1, concat_axis=1, tiled=...]
    all_to_all x1 -> x0, starting transfers between devices: 3.93 us -> none  [local(): lax.all_to_all(token_gradient, 'var', split_axis=1, concat_axis=1, tiled=...]
    reshape x2 -> x3, local copies, waits for them, and re-layouts: 3.22 us -> 0.14 us  [the longest x2 0.09 us: local(): (kernels.astype(jnp.float32) * own_member[:, None, None]).reshape(var_loc...]
    all_to_all x1, starting transfers between devices: 18.5 us -> 17.4 us  [local(): lax.all_to_all(pieces, 'dp', split_axis=0, concat_axis=0, tiled=True)]
    mul x1, other arithmetic: 0.08 us -> 0.92 us  [local(): kernels.astype(jnp.float32) * own_member[:, None, None]]
    reduce_sum x1, other arithmetic: 0.6 us -> 1.42 us  [level_tables(): inv = 1.0 / jnp.maximum(jnp.sum(onehot, axis=1), 1.0)]
    unnamed x16 -> x12, local copies, waits for them, and re-layouts: 1.8 us -> 1.79 us
  transfers between devices with their start and end apart: 3 -> 2, of which waited for: 3 -> 2; matrix products, arithmetic and copies ran while one was open for 10% -> 10% of each run, Pallas kernels for 0% -> 0%
where the time goes in v5:
time: 77.7 us; the launch traced here: 77.2 us
  starting transfers between devices  26.4 us (34%)
  waiting for transfers between devices  16.8 us (22%)
  blocking collectives  13.4 us (17%)
  matrix products  11.2 us (14%)
  other arithmetic  4.46 us (6%)
  local copies, waits for them, and re-layouts  3.44 us (4%)
  between operations  1.52 us (2%)
    all_to_all x1, starting transfers between devices, local(): lax.all_to_all(pieces, 'dp', split_axis=0, concat_axis=0, tiled=True)  17.4 us
    all_to_all x1, blocking collectives, local(): lax.all_to_all(token_gradient, 'var', split_axis=1, concat_axis=1, tiled=...  13.4 us
    all_to_all x1, waiting for transfers between devices, local(): lax.all_to_all(pieces, 'dp', split_axis=0, concat_axis=0, tiled=True)  10.8 us
    all_to_all x1, starting transfers between devices, local(): lax.all_to_all(token_rows, 'var', split_axis=1, concat_axis=1, tiled=True)  9 us
    all_to_all x1, waiting for transfers between devices, local(): lax.all_to_all(token_rows, 'var', split_axis=1, concat_axis=1, tiled=True)  5.96 us
    dot_general x1, matrix products, block_pass(): jnp.dot(hidden, w_out, preferred_element_type=jnp.float32)  3.76 us
    dot_general x1, matrix products, block_pass(): jnp.dot(gradient_rows, w_out.T, preferred_element_type=jnp.float32)  3.69 us
    unnamed x12, local copies, waits for them, and re-layouts  1.79 us
  transfers between devices with their start and end apart: 2, of which 2 were waited for; matrix products, arithmetic and copies ran while one was open for 10% of the time, Pallas kernels for 0%

profile of v5, /device:TPU:1, one launch (start us, length us, event | category | flops | bytes accessed | tf_op | source)
XLA Modules:
  0.0 77.2 jit_solution(8166250842631591944)
XLA Ops:
  0.7 1.4 %convert_reduce_fusion.2 = f32[]{:T(128)} fusion(s32[4]{0:T(128)} %param.9), kind=kLoop, calls=%fused_computation.35 | loop fusion | flops 7 | bytes 20 | tf_op jit(solution)/shard_map/reduce_sum | solution.py:53
  2.8 0.7 broadcast_multiply_fusion.4
  3.4 0.9 %convert_multiply_fusion = f32[4,16,512]{2,1,0:T(8,128)S(1)} fusion(bf16[4,16,512]{2,1,0:T(8,128)(2,1)} %param.8, f32[4]{0:T(128)S(1)} %get-tuple-element.5), kind=kLoop, calls=%fused_computation.27 | loop fusion | flops 65536 | bytes 196624 | tf_op jit(solution)/shard_map/mul | solution.py:73
  4.5 0.8 copy.21
  5.3 0.2 copy.22
  5.5 0.2 reshape.110
  5.6 1.1 %convolution_convert_fusion = bf16[512,256]{0,1:T(8,128)(2,1)} fusion(f32[64,512]{1,0:T(8,128)S(1)} %reshape.107, bf16[256,64]{1,0:T(8,128)(2,1)S(1)} %reshape.110), kind=kOutput, calls=%fused_computation.13 | convolution fusion | flops 100794368 | bytes 425984 | tf_op jit(solution)/shard_map/bnk,ke->bne/dot_general | solution.py:75
  6.7 9.0 %all-to-all-start = ((bf16[1,16,16,512]{3,2,0,1:T(8,128)(2,1)}), bf16[1,16,16,512]{3,2,0,1:T(8,128)(2,1)S(1)}, u32[]{:S(2)}, u32[]{:S(2)}) async-start(bf16[1,16,16,512]{3,2,0,1:T(8,128)(2,1)} %bitcast.7), calls=%async_computation | async-start | bytes 524288 | tf_op jit(solution)/shard_map/all_to_all | solution.py:84
  15.8 3.7 %fusion.26 = f32[256,2048]{1,0:T(8,128)} fusion(bf16[256,512]{1,0:T(8,128)(2,1)S(1)} %bitcast.55, bf16[2048,512]{1,0:T(8,128)(2,1)} %param.12), kind=kOutput, calls=%fused_computation.49 | convolution fusion | flops 536870912 | bytes 4456448 | tf_op jit(solution)/shard_map/dot_general | solution.py:33
  19.4 6.0 %all-to-all-done = bf16[1,16,16,512]{3,2,0,1:T(8,128)(2,1)S(1)} async-done(((bf16[1,16,16,512]{3,2,0,1:T(8,128)(2,1)}), bf16[1,16,16,512]{3,2,0,1:T(8,128)(2,1)S(1)}, u32[]{:S(2)}, u32[]{:S(2)}) %all-to-all-start) | async-done | bytes 262176 | tf_op jit(solution)/shard_map/all_to_all | solution.py:84
  25.6 0.2 multiply_reduce_fusion.1
  25.9 0.1 multiply_convert_fusion.2
  26.1 0.7 fusion.25
  26.8 0.9 %copy-done.2 = f32[256,2048]{1,0:T(8,128)S(1)} copy-done((f32[256,2048]{1,0:T(8,128)S(1)}, f32[256,2048]{1,0:T(8,128)}, u32[]{:S(2)}) %copy-start.2) | copy-done | bytes 2097176
  27.7 1.8 %fusion.24 = (f32[256]{0:T(256)S(1)}, f32[256]{0:T(256)S(1)}, f32[256,512]{1,0:T(8,128)S(1)}) fusion(f32[256]{0:T(256)S(1)} %rsqrt.12, f32[256]{0:T(256)S(1)} %div.20, bf16[1,16,16,512]{3,2,0,1:T(8,128)(2,1)S(1)} %all-to-all-done, f32[512]{0:T(512)S(1)} %copy-done.4, bf16[512,2048]{1,0:T(8,128)(2,1)S(1)} %copy-done, f32[256,2048]{1,0:T(8,128)S(1)} %fusion.25, ...), kind=kOutput, calls=%fused_computation.47 | convolution fusion | flops 548273664 | bytes 7084032 | tf_op jit(solution)/shard_map/dot_general | solution.py:36
  29.5 0.2 add_convert_fusion
  29.7 13.4 %all_to_all.15 = bf16[1,16,16,512]{3,2,0,1:T(8,128)(2,1)S(1)} all-to-all(bf16[1,16,16,512]{3,2,0,1:T(8,128)(2,1)S(1)} %bitcast.56), channel_id=1, replica_groups=mesh['var'=16,'dp'=32] {'var'}, dimensions={1} | all-to-all | bytes 524288 | tf_op jit(solution)/shard_map/all_to_all | solution.py:86
  43.3 0.2 convolution_convert_fusion.1
  43.5 0.8 reshape.120
  44.3 17.4 %all-to-all-start.2 = ((bf16[32,2,512]{2,1,0:T(2,128)(2,1)}), bf16[32,2,512]{2,1,0:T(2,128)(2,1)S(1)}, u32[]{:S(2)}, u32[]{:S(2)}) async-start(bf16[32,2,512]{2,1,0:T(2,128)(2,1)} %reshape.120), calls=%async_computation.2 | async-start | bytes 131072 | tf_op jit(solution)/shard_map/all_to_all | solution.py:90
  61.7 3.8 %fusion.7 = bf16[256,512]{1,0:T(8,128)(2,1)} fusion(bf16[2048,512]{1,0:T(8,128)(2,1)} %param.12, f32[256,2048]{1,0:T(8,128)} %copy-done.1, bf16[256,512]{1,0:T(8,128)(2,1)S(1)} %bitcast.54), kind=kOutput, calls=%fused_computation.12 | convolution fusion | flops 541982720 | bytes 4718592 | tf_op jit(solution)/shard_map/dot_general | solution.py:29
  65.4 10.8 %all-to-all-done.2 = bf16[32,2,512]{2,1,0:T(2,128)(2,1)S(1)} async-done(((bf16[32,2,512]{2,1,0:T(2,128)(2,1)}), bf16[32,2,512]{2,1,0:T(2,128)(2,1)S(1)}, u32[]{:S(2)}, u32[]{:S(2)}) %all-to-all-start.2) | async-done | bytes 65568 | tf_op jit(solution)/shard_map/all_to_all | solution.py:90
  76.2 0.1 reshape.121
  76.5 0.7 broadcast_multiply_fusion
  (22 shorter events, 0.7 us)
Async XLA Ops:
  0.6 25.4 %copy-start = (bf16[512,2048]{1,0:T(8,128)(2,1)S(1)}, bf16[512,2048]{1,0:T(8,128)(2,1)}, u32[]{:S(2)}) copy-start(bf16[512,2048]{1,0:T(8,128)(2,1)} %param.11) | copy-start | bytes 6291460
  0.6 15.1 %copy-start.3 = (bf16[1,16,16,512]{3,2,1,0:T(8,128)(2,1)S(1)}, bf16[1,16,16,512]{3,2,1,0:T(8,128)(2,1)}, u32[]{:S(2)}) copy-start(bf16[1,16,16,512]{3,2,1,0:T(8,128)(2,1)} %param.13) | copy-start | bytes 786436
  6.7 18.7 %all-to-all-start = ((bf16[1,16,16,512]{3,2,0,1:T(8,128)(2,1)}), bf16[1,16,16,512]{3,2,0,1:T(8,128)(2,1)S(1)}, u32[]{:S(2)}, u32[]{:S(2)}) async-start(bf16[1,16,16,512]{3,2,0,1:T(8,128)(2,1)} %bitcast.7), calls=%async_computation | async-start | bytes 524288 | tf_op jit(solution)/shard_map/all_to_all | solution.py:84
  15.7 10.2 %copy-start.4 = (f32[512]{0:T(512)S(1)}, f32[512]{0:T(512)}, u32[]{:S(2)}) copy-start(f32[512]{0:T(512)} %param.10) | copy-start | bytes 6148
  26.1 1.6 %copy-start.2 = (f32[256,2048]{1,0:T(8,128)S(1)}, f32[256,2048]{1,0:T(8,128)}, u32[]{:S(2)}) copy-start(f32[256,2048]{1,0:T(8,128)} %fusion.26) | copy-start | bytes 6291460
  27.7 1.8 %copy-start.1 = (f32[256,2048]{1,0:T(8,128)}, f32[256,2048]{1,0:T(8,128)S(1)}, u32[]{:S(2)}) copy-start(f32[256,2048]{1,0:T(8,128)S(1)} %fusion.25) | copy-start | bytes 6291460
  44.3 32.0 %all-to-all-start.2 = ((bf16[32,2,512]{2,1,0:T(2,128)(2,1)}), bf16[32,2,512]{2,1,0:T(2,128)(2,1)S(1)}, u32[]{:S(2)}, u32[]{:S(2)}) async-start(bf16[32,2,512]{2,1,0:T(2,128)(2,1)} %reshape.120), calls=%async_computation.2 | async-start | bytes 131072 | tf_op jit(solution)/shard_map/all_to_all | solution.py:90

commit v6 on v5

--- a/solution.py
+++ b/solution.py
@@ -76,7 +76,7 @@
         "bnk,ke->bne",
         rows.astype(jnp.float32),
         weighted,
-        precision=lax.Precision.HIGHEST,
+        precision=lax.Precision.HIGH,
         preferred_element_type=jnp.float32,
     ).astype(jnp.bfloat16)
     chunks = lax.axis_size("var")

time: 77.7 us -> 77.6 us (level)
  no operation moved by 1% of the time
where the time goes in v6:
time: 77.6 us; the launch traced here: 77.1 us
  starting transfers between devices  26.4 us (34%)
  waiting for transfers between devices  16.8 us (22%)
  blocking collectives  13.4 us (17%)
  matrix products  11.1 us (14%)
  other arithmetic  4.46 us (6%)
  local copies, waits for them, and re-layouts  3.44 us (4%)
  between operations  1.52 us (2%)
    all_to_all x1, starting transfers between devices, local(): lax.all_to_all(pieces, 'dp', split_axis=0, concat_axis=0, tiled=True)  17.4 us
    all_to_all x1, blocking collectives, local(): lax.all_to_all(token_gradient, 'var', split_axis=1, concat_axis=1, tiled=...  13.4 us
    all_to_all x1, waiting for transfers between devices, local(): lax.all_to_all(pieces, 'dp', split_axis=0, concat_axis=0, tiled=True)  10.8 us
    all_to_all x1, starting transfers between devices, local(): lax.all_to_all(token_rows, 'var', split_axis=1, concat_axis=1, tiled=True)  9 us
    all_to_all x1, waiting for transfers between devices, local(): lax.all_to_all(token_rows, 'var', split_axis=1, concat_axis=1, tiled=True)  5.96 us
    dot_general x1, matrix products, block_pass(): jnp.dot(hidden, w_out, preferred_element_type=jnp.float32)  3.76 us
    dot_general x1, matrix products, block_pass(): jnp.dot(gradient_rows, w_out.T, preferred_element_type=jnp.float32)  3.69 us
    unnamed x12, local copies, waits for them, and re-layouts  1.79 us
  transfers between devices with their start and end apart: 2, of which 2 were waited for; matrix products, arithmetic and copies ran while one was open for 10% of the time, Pallas kernels for 0%

profile of v6, /device:TPU:1, one launch (start us, length us, event | category | flops | bytes accessed | tf_op | source)
XLA Modules:
  0.0 77.1 jit_solution(12831980579795905035)
XLA Ops:
  0.7 1.4 %convert_reduce_fusion.2 = f32[]{:T(128)} fusion(s32[4]{0:T(128)} %param.9), kind=kLoop, calls=%fused_computation.35 | loop fusion | flops 7 | bytes 20 | tf_op jit(solution)/shard_map/reduce_sum | solution.py:53
  2.8 0.7 broadcast_multiply_fusion.4
  3.4 0.9 %convert_multiply_fusion = f32[4,16,512]{2,1,0:T(8,128)S(1)} fusion(bf16[4,16,512]{2,1,0:T(8,128)(2,1)} %param.8, f32[4]{0:T(128)S(1)} %get-tuple-element.5), kind=kLoop, calls=%fused_computation.27 | loop fusion | flops 65536 | bytes 196624 | tf_op jit(solution)/shard_map/mul | solution.py:73
  4.5 0.8 copy.21
  5.3 0.2 copy.22
  5.5 0.2 reshape.110
  5.6 1.0 %convolution_convert_fusion = bf16[512,256]{0,1:T(8,128)(2,1)} fusion(f32[64,512]{1,0:T(8,128)S(1)} %reshape.107, bf16[256,64]{1,0:T(8,128)(2,1)S(1)} %reshape.110), kind=kOutput, calls=%fused_computation.13 | convolution fusion | flops 50462720 | bytes 425984 | tf_op jit(solution)/shard_map/bnk,ke->bne/dot_general | solution.py:75
  6.6 9.0 %all-to-all-start = ((bf16[1,16,16,512]{3,2,0,1:T(8,128)(2,1)}), bf16[1,16,16,512]{3,2,0,1:T(8,128)(2,1)S(1)}, u32[]{:S(2)}, u32[]{:S(2)}) async-start(bf16[1,16,16,512]{3,2,0,1:T(8,128)(2,1)} %bitcast.7), calls=%async_computation | async-start | bytes 524288 | tf_op jit(solution)/shard_map/all_to_all | solution.py:84
  15.7 3.7 %fusion.26 = f32[256,2048]{1,0:T(8,128)} fusion(bf16[256,512]{1,0:T(8,128)(2,1)S(1)} %bitcast.55, bf16[2048,512]{1,0:T(8,128)(2,1)} %param.12), kind=kOutput, calls=%fused_computation.49 | convolution fusion | flops 536870912 | bytes 4456448 | tf_op jit(solution)/shard_map/dot_general | solution.py:33
  19.4 6.0 %all-to-all-done = bf16[1,16,16,512]{3,2,0,1:T(8,128)(2,1)S(1)} async-done(((bf16[1,16,16,512]{3,2,0,1:T(8,128)(2,1)}), bf16[1,16,16,512]{3,2,0,1:T(8,128)(2,1)S(1)}, u32[]{:S(2)}, u32[]{:S(2)}) %all-to-all-start) | async-done | bytes 262176 | tf_op jit(solution)/shard_map/all_to_all | solution.py:84
  25.5 0.2 multiply_reduce_fusion.1
  25.8 0.1 multiply_convert_fusion.2
  26.0 0.7 fusion.25
  26.7 0.9 %copy-done.2 = f32[256,2048]{1,0:T(8,128)S(1)} copy-done((f32[256,2048]{1,0:T(8,128)S(1)}, f32[256,2048]{1,0:T(8,128)}, u32[]{:S(2)}) %copy-start.2) | copy-done | bytes 2097176
  27.6 1.8 %fusion.24 = (f32[256]{0:T(256)S(1)}, f32[256]{0:T(256)S(1)}, f32[256,512]{1,0:T(8,128)S(1)}) fusion(f32[256]{0:T(256)S(1)} %rsqrt.12, f32[256]{0:T(256)S(1)} %div.20, bf16[1,16,16,512]{3,2,0,1:T(8,128)(2,1)S(1)} %all-to-all-done, f32[512]{0:T(512)S(1)} %copy-done.4, bf16[512,2048]{1,0:T(8,128)(2,1)S(1)} %copy-done, f32[256,2048]{1,0:T(8,128)S(1)} %fusion.25, ...), kind=kOutput, calls=%fused_computation.47 | convolution fusion | flops 548273664 | bytes 7084032 | tf_op jit(solution)/shard_map/dot_general | solution.py:36
  29.4 0.2 add_convert_fusion
  29.7 13.4 %all_to_all.15 = bf16[1,16,16,512]{3,2,0,1:T(8,128)(2,1)S(1)} all-to-all(bf16[1,16,16,512]{3,2,0,1:T(8,128)(2,1)S(1)} %bitcast.56), channel_id=1, replica_groups=mesh['var'=16,'dp'=32] {'var'}, dimensions={1} | all-to-all | bytes 524288 | tf_op jit(solution)/shard_map/all_to_all | solution.py:86
  43.2 0.2 convolution_convert_fusion.1
  43.4 0.8 reshape.120
  44.2 17.4 %all-to-all-start.2 = ((bf16[32,2,512]{2,1,0:T(2,128)(2,1)}), bf16[32,2,512]{2,1,0:T(2,128)(2,1)S(1)}, u32[]{:S(2)}, u32[]{:S(2)}) async-start(bf16[32,2,512]{2,1,0:T(2,128)(2,1)} %reshape.120), calls=%async_computation.2 | async-start | bytes 131072 | tf_op jit(solution)/shard_map/all_to_all | solution.py:90
  61.6 3.8 %fusion.7 = bf16[256,512]{1,0:T(8,128)(2,1)} fusion(bf16[2048,512]{1,0:T(8,128)(2,1)} %param.12, f32[256,2048]{1,0:T(8,128)} %copy-done.1, bf16[256,512]{1,0:T(8,128)(2,1)S(1)} %bitcast.54), kind=kOutput, calls=%fused_computation.12 | convolution fusion | flops 541982720 | bytes 4718592 | tf_op jit(solution)/shard_map/dot_general | solution.py:29
  65.4 10.8 %all-to-all-done.2 = bf16[32,2,512]{2,1,0:T(2,128)(2,1)S(1)} async-done(((bf16[32,2,512]{2,1,0:T(2,128)(2,1)}), bf16[32,2,512]{2,1,0:T(2,128)(2,1)S(1)}, u32[]{:S(2)}, u32[]{:S(2)}) %all-to-all-start.2) | async-done | bytes 65568 | tf_op jit(solution)/shard_map/all_to_all | solution.py:90
  76.2 0.1 reshape.121
  76.5 0.7 broadcast_multiply_fusion
  (22 shorter events, 0.7 us)
Async XLA Ops:
  0.6 25.4 %copy-start = (bf16[512,2048]{1,0:T(8,128)(2,1)S(1)}, bf16[512,2048]{1,0:T(8,128)(2,1)}, u32[]{:S(2)}) copy-start(bf16[512,2048]{1,0:T(8,128)(2,1)} %param.11) | copy-start | bytes 6291460
  0.6 15.0 %copy-start.3 = (bf16[1,16,16,512]{3,2,1,0:T(8,128)(2,1)S(1)}, bf16[1,16,16,512]{3,2,1,0:T(8,128)(2,1)}, u32[]{:S(2)}) copy-start(bf16[1,16,16,512]{3,2,1,0:T(8,128)(2,1)} %param.13) | copy-start | bytes 786436
  6.6 18.7 %all-to-all-start = ((bf16[1,16,16,512]{3,2,0,1:T(8,128)(2,1)}), bf16[1,16,16,512]{3,2,0,1:T(8,128)(2,1)S(1)}, u32[]{:S(2)}, u32[]{:S(2)}) async-start(bf16[1,16,16,512]{3,2,0,1:T(8,128)(2,1)} %bitcast.7), calls=%async_computation | async-start | bytes 524288 | tf_op jit(solution)/shard_map/all_to_all | solution.py:84
  15.7 10.2 %copy-start.4 = (f32[512]{0:T(512)S(1)}, f32[512]{0:T(512)}, u32[]{:S(2)}) copy-start(f32[512]{0:T(512)} %param.10) | copy-start | bytes 6148
  26.0 1.6 %copy-start.2 = (f32[256,2048]{1,0:T(8,128)S(1)}, f32[256,2048]{1,0:T(8,128)}, u32[]{:S(2)}) copy-start(f32[256,2048]{1,0:T(8,128)} %fusion.26) | copy-start | bytes 6291460
  27.6 1.8 %copy-start.1 = (f32[256,2048]{1,0:T(8,128)}, f32[256,2048]{1,0:T(8,128)S(1)}, u32[]{:S(2)}) copy-start(f32[256,2048]{1,0:T(8,128)S(1)} %fusion.25) | copy-start | bytes 6291460
  44.2 32.0 %all-to-all-start.2 = ((bf16[32,2,512]{2,1,0:T(2,128)(2,1)}), bf16[32,2,512]{2,1,0:T(2,128)(2,1)S(1)}, u32[]{:S(2)}, u32[]{:S(2)}) async-start(bf16[32,2,512]{2,1,0:T(2,128)(2,1)} %reshape.120), calls=%async_computation.2 | async-start | bytes 131072 | tf_op jit(solution)/shard_map/all_to_all | solution.py:90

commit v7 on v6

--- a/solution.py
+++ b/solution.py
@@ -30,7 +30,7 @@
         jnp.bfloat16
     )
     gradient_rows = grads.reshape(-1, width)
-    dhid = lax.optimization_barrier(jnp.dot(gradient_rows, w_out.T, preferred_element_type=jnp.float32))
+    dhid = lax.optimization_barrier(jnp.dot(gradient_rows, w_out.T, preferred_element_type=jnp.float32).astype(jnp.bfloat16)).astype(jnp.float32)
     gelu_back = jax.vjp(lambda value: jax.nn.gelu(value, approximate=True), pre)[1]
     dpre = gelu_back(dhid)[0].astype(jnp.bfloat16)
     dnorm = jnp.dot(dpre, w_in.T, preferred_element_type=jnp.float32)

time: 77.6 us -> 76.8 us (0.990)
  waiting for transfers between devices: 16.8 us -> 18 us
  matrix products: 11.1 us -> 9.95 us
  local copies, waits for them, and re-layouts: 3.44 us -> 2.57 us
    all_to_all x1, waiting for transfers between devices: 5.96 us -> 7.21 us  [local(): lax.all_to_all(token_rows, 'var', split_axis=1, concat_axis=1, tiled=True)]
    dot_general x1, matrix products: 3.69 us -> 2.43 us  [block_pass(): jnp.dot(gradient_rows, w_out.T, preferred_element_type=jnp.float32)]
    unnamed x12 -> x10, local copies, waits for them, and re-layouts: 1.79 us -> 0.92 us
  transfers between devices with their start and end apart: 2 -> 2, of which waited for: 2 -> 2; matrix products, arithmetic and copies ran while one was open for 10% -> 8% of each run, Pallas kernels for 0% -> 0%
where the time goes in v7:
time: 76.8 us; the launch traced here: 76.3 us
  starting transfers between devices  26.4 us (34%)
  waiting for transfers between devices  18 us (23%)
  blocking collectives  13.4 us (17%)
  matrix products  9.95 us (13%)
  other arithmetic  4.45 us (6%)
  local copies, waits for them, and re-layouts  2.57 us (3%)
  between operations  1.53 us (2%)
    all_to_all x1, starting transfers between devices, local(): lax.all_to_all(pieces, 'dp', split_axis=0, concat_axis=0, tiled=True)  17.4 us
    all_to_all x1, blocking collectives, local(): lax.all_to_all(token_gradient, 'var', split_axis=1, concat_axis=1, tiled=...  13.4 us
    all_to_all x1, waiting for transfers between devices, local(): lax.all_to_all(pieces, 'dp', split_axis=0, concat_axis=0, tiled=True)  10.8 us
    all_to_all x1, starting transfers between devices, local(): lax.all_to_all(token_rows, 'var', split_axis=1, concat_axis=1, tiled=True)  9 us
    all_to_all x1, waiting for transfers between devices, local(): lax.all_to_all(token_rows, 'var', split_axis=1, concat_axis=1, tiled=True)  7.21 us
    dot_general x1, matrix products, block_pass(): jnp.dot(hidden, w_out, preferred_element_type=jnp.float32)  3.76 us
    dot_general x1, matrix products, block_pass(): jnp.dot(gradient_rows, w_out.T, preferred_element_type=jnp.float32)  2.43 us
    dot_general x1, matrix products, block_pass(): dnorm = jnp.dot(dpre, w_in.T, preferred_element_type=jnp.float32)  1.83 us
  transfers between devices with their start and end apart: 2, of which 2 were waited for; matrix products, arithmetic and copies ran while one was open for 8% of the time, Pallas kernels for 0%

profile of v7, /device:TPU:1, one launch (start us, length us, event | category | flops | bytes accessed | tf_op | source)
XLA Modules:
  0.0 76.3 jit_solution(16628280272532963966)
XLA Ops:
  0.6 1.4 %convert_reduce_fusion.2 = f32[]{:T(128)} fusion(s32[4]{0:T(128)} %param.9), kind=kLoop, calls=%fused_computation.41 | loop fusion | flops 7 | bytes 20 | tf_op jit(solution)/shard_map/reduce_sum | solution.py:53
  2.7 0.7 broadcast_multiply_fusion.4
  3.4 0.8 %copy.21 = bf16[1,8,4,4,128]{4,1,3,2,0:T(8,128)(2,1)S(1)} copy(bf16[1,8,4,4,128]{4,3,1,2,0:T(4,128)(2,1)} %bitcast.64) | data formatting | bytes 65536 | tf_op jit(solution)/shard_map/transpose | solution.py:60
  4.2 0.9 %convert_multiply_fusion.2 = f32[4,16,512]{2,1,0:T(8,128)S(1)} fusion(bf16[4,16,512]{2,1,0:T(8,128)(2,1)} %param.8, f32[4]{0:T(128)S(1)} %get-tuple-element.5), kind=kLoop, calls=%fused_computation.33 | loop fusion | flops 65536 | bytes 196624 | tf_op jit(solution)/shard_map/mul | solution.py:73
  5.3 0.2 copy.22
  5.4 0.2 reshape.110
  5.6 1.0 %convolution_convert_fusion.1 = bf16[512,256]{0,1:T(8,128)(2,1)} fusion(f32[64,512]{1,0:T(8,128)S(1)} %reshape.107, bf16[256,64]{1,0:T(8,128)(2,1)S(1)} %reshape.110), kind=kOutput, calls=%fused_computation.19 | convolution fusion | flops 50462720 | bytes 425984 | tf_op jit(solution)/shard_map/bnk,ke->bne/dot_general | solution.py:75
  6.6 9.0 %all-to-all-start = ((bf16[1,16,16,512]{3,2,0,1:T(8,128)(2,1)}), bf16[1,16,16,512]{3,2,0,1:T(8,128)(2,1)S(1)}, u32[]{:S(2)}, u32[]{:S(2)}) async-start(bf16[1,16,16,512]{3,2,0,1:T(8,128)(2,1)} %bitcast.7), calls=%async_computation | async-start | bytes 524288 | tf_op jit(solution)/shard_map/all_to_all | solution.py:84
  15.6 2.4 %convolution_convert_fusion = bf16[256,2048]{1,0:T(8,128)(2,1)S(1)} fusion(bf16[256,512]{1,0:T(8,128)(2,1)} %bitcast.58, bf16[2048,512]{1,0:T(8,128)(2,1)} %param.12), kind=kOutput, calls=%fused_computation.4 | convolution fusion | flops 537395200 | bytes 3407872 | tf_op jit(solution)/shard_map/dot_general | solution.py:33
  18.1 7.2 %all-to-all-done = bf16[1,16,16,512]{3,2,0,1:T(8,128)(2,1)S(1)} async-done(((bf16[1,16,16,512]{3,2,0,1:T(8,128)(2,1)}), bf16[1,16,16,512]{3,2,0,1:T(8,128)(2,1)S(1)}, u32[]{:S(2)}, u32[]{:S(2)}) %all-to-all-start) | async-done | bytes 262176 | tf_op jit(solution)/shard_map/all_to_all | solution.py:84
  25.5 0.2 multiply_reduce_fusion.1
  25.8 0.1 multiply_convert_fusion.2
  26.0 0.7 fusion.28
  26.7 1.8 %fusion.27 = (f32[256]{0:T(256)S(1)}, f32[256]{0:T(256)S(1)}, f32[256,512]{1,0:T(8,128)S(1)}) fusion(f32[256]{0:T(256)S(1)} %rsqrt.12, f32[256]{0:T(256)S(1)} %div.20, bf16[1,16,16,512]{3,2,0,1:T(8,128)(2,1)S(1)} %all-to-all-done, f32[512]{0:T(512)S(1)} %copy-done.3, bf16[512,2048]{1,0:T(8,128)(2,1)S(1)} %copy-done, ...), kind=kOutput, calls=%fused_computation.53 | convolution fusion | flops 548797952 | bytes 6035456 | tf_op jit(solution)/shard_map/dot_general | solution.py:36
  28.6 0.3 add_convert_fusion
  28.8 13.4 %all_to_all.15 = bf16[1,16,16,512]{3,2,0,1:T(8,128)(2,1)S(1)} all-to-all(bf16[1,16,16,512]{3,2,0,1:T(8,128)(2,1)S(1)} %bitcast.55), channel_id=1, replica_groups=mesh['var'=16,'dp'=32] {'var'}, dimensions={1} | all-to-all | bytes 524288 | tf_op jit(solution)/shard_map/all_to_all | solution.py:86
  42.2 0.1 copy.25
  42.4 0.2 convolution_convert_fusion.2
  42.6 0.8 reshape.120
  43.4 17.4 %all-to-all-start.2 = ((bf16[32,2,512]{2,1,0:T(2,128)(2,1)}), bf16[32,2,512]{2,1,0:T(2,128)(2,1)S(1)}, u32[]{:S(2)}, u32[]{:S(2)}) async-start(bf16[32,2,512]{2,1,0:T(2,128)(2,1)} %reshape.120), calls=%async_computation.2 | async-start | bytes 131072 | tf_op jit(solution)/shard_map/all_to_all | solution.py:90
  60.8 3.8 %fusion.10 = bf16[256,512]{1,0:T(8,128)(2,1)} fusion(bf16[2048,512]{1,0:T(8,128)(2,1)} %param.12, f32[256,2048]{1,0:T(8,128)} %copy-done.1, bf16[256,512]{1,0:T(8,128)(2,1)S(1)} %bitcast.54), kind=kOutput, calls=%fused_computation.18 | convolution fusion | flops 541982720 | bytes 4718592 | tf_op jit(solution)/shard_map/dot_general | solution.py:29
  64.5 10.8 %all-to-all-done.2 = bf16[32,2,512]{2,1,0:T(2,128)(2,1)S(1)} async-done(((bf16[32,2,512]{2,1,0:T(2,128)(2,1)}), bf16[32,2,512]{2,1,0:T(2,128)(2,1)S(1)}, u32[]{:S(2)}, u32[]{:S(2)}) %all-to-all-start.2) | async-done | bytes 65568 | tf_op jit(solution)/shard_map/all_to_all | solution.py:90
  75.3 0.1 reshape.121
  75.6 0.7 broadcast_multiply_fusion
  (20 shorter events, 0.6 us)
Async XLA Ops:
  0.6 25.3 %copy-start = (bf16[512,2048]{1,0:T(8,128)(2,1)S(1)}, bf16[512,2048]{1,0:T(8,128)(2,1)}, u32[]{:S(2)}) copy-start(bf16[512,2048]{1,0:T(8,128)(2,1)} %param.11) | copy-start | bytes 6291460
  6.6 18.7 %all-to-all-start = ((bf16[1,16,16,512]{3,2,0,1:T(8,128)(2,1)}), bf16[1,16,16,512]{3,2,0,1:T(8,128)(2,1)S(1)}, u32[]{:S(2)}, u32[]{:S(2)}) async-start(bf16[1,16,16,512]{3,2,0,1:T(8,128)(2,1)} %bitcast.7), calls=%async_computation | async-start | bytes 524288 | tf_op jit(solution)/shard_map/all_to_all | solution.py:84
  15.6 10.2 %copy-start.3 = (f32[512]{0:T(512)S(1)}, f32[512]{0:T(512)}, u32[]{:S(2)}) copy-start(f32[512]{0:T(512)} %param.10) | copy-start | bytes 6148
  26.7 1.9 %copy-start.1 = (f32[256,2048]{1,0:T(8,128)}, f32[256,2048]{1,0:T(8,128)S(1)}, u32[]{:S(2)}) copy-start(f32[256,2048]{1,0:T(8,128)S(1)} %fusion.28) | copy-start | bytes 6291460
  26.7 1.9 %copy-start.2 = (bf16[1,16,16,512]{3,2,1,0:T(8,128)(2,1)S(1)}, bf16[1,16,16,512]{3,2,1,0:T(8,128)(2,1)}, u32[]{:S(2)}) copy-start(bf16[1,16,16,512]{3,2,1,0:T(8,128)(2,1)} %param.13) | copy-start | bytes 786436
  43.4 32.0 %all-to-all-start.2 = ((bf16[32,2,512]{2,1,0:T(2,128)(2,1)}), bf16[32,2,512]{2,1,0:T(2,128)(2,1)S(1)}, u32[]{:S(2)}, u32[]{:S(2)}) async-start(bf16[32,2,512]{2,1,0:T(2,128)(2,1)} %reshape.120), calls=%async_computation.2 | async-start | bytes 131072 | tf_op jit(solution)/shard_map/all_to_all | solution.py:90
